TPU v7x, 256 devices: a whole 4x4x8 slice. The times are simulated.
256 devices in a mesh: ctx: 32 (over x, z), head: 8 (over y, core).
Axes of the slice: x: 4, y: 4, z: 8, core: 2. Of those that a mesh axis runs over, the one named last changes fastest.
Arguments:
- query_in: bfloat16 [16384, 2048], P('ctx', 'head'), may hold values from -6 to 6
- key_in: bfloat16 [16384, 2048], P('ctx', 'head'), may hold values from -6 to 6
- value_in: bfloat16 [16384, 4096], P('ctx', 'head'), may hold values from -6 to 6
- query_taps: float32 [4, 2048], P(None, 'head'), may hold values from -3 to 3
- key_taps: float32 [4, 2048], P(None, 'head'), may hold values from -3 to 3
- value_taps: float32 [4, 4096], P(None, 'head'), may hold values from -3 to 3
- log_decay: float32 [32, 16384], P('head', 'ctx'), may hold values from -2 to 0
- beta_logit: float32 [32, 16384], P('head', 'ctx'), may hold values from -9 to 2
- gate_in: bfloat16 [16384, 4096], P('ctx', 'head'), may hold values from -6 to 6
- norm_gain: float32 [128], replicated, may hold values from 0.1 to 1.9
Outputs:
- core_out: bfloat16 [16384, 4096], P(('ctx', 'head'))
All inputs are finite; a program needn't handle non-finite values.
Results may differ from a plain program's by a relative error of at most 0.005.
Values may be sent and summed in bfloat16 or wider, within the bound.
No kernel may reach another device: no remote copies, remote signals or barrier semaphores. Data moves between devices by JAX's collectives and lax.ppermute only.
A program may use at most 64 MiB of HBM per device.

v0:
```python
import jax
import jax.numpy as jnp
from jax import lax
from jax.sharding import PartitionSpec as P

GROUP = 64


highest = lax.Precision.HIGHEST
high = lax.Precision.HIGH
norm_eps = 1e-06


def shifted(value, axis, steps):
    count = lax.axis_size(axis)
    first, last = (max(0, -steps), min(count, count - steps))
    return lax.ppermute(value, axis, [(source, source + steps) for source in range(first, last)])


def causal_conv(joined, taps, length):
    summed = jnp.zeros((length, joined.shape[1]), jnp.float32)
    for offset in range(taps.shape[0]):
        summed = summed + taps[offset] * joined[offset : offset + length].astype(jnp.float32)
    return jax.nn.silu(summed)


def unit_rows(matrix):
    return matrix * lax.rsqrt(jnp.sum(matrix * matrix, axis=-1, keepdims=True) + norm_eps)


def unit_lower_inverse(strict, row_ids, col_ids):
    length = strict.shape[-1]
    eye = (row_ids == col_ids).astype(jnp.float32)
    inverse = eye - jnp.where(row_ids // 2 == col_ids // 2, strict, 0.0)

    def level(depth, inverse):
        width = 2 << depth
        lower_left = jnp.where(
            (row_ids // (2 * width) == col_ids // (2 * width)) & (row_ids // width != col_ids // width),
            strict,
            0.0,
        )
        return inverse - matmul_pair(matmul_pair(inverse, lower_left, highest), inverse, highest)

    return lax.fori_loop(0, length.bit_length() - 2, level, inverse)


def group_terms(query, keys, values, beta, logdecay):
    length = logdecay.shape[-1]
    cumul = jnp.cumsum(logdecay, axis=-1)
    row_ids = lax.broadcasted_iota(jnp.int32, (length, length), 0)
    col_ids = lax.broadcasted_iota(jnp.int32, (length, length), 1)
    inside = col_ids <= row_ids
    differ = cumul[..., :, None] - cumul[..., None, :]
    decay_mask = jnp.where(inside, jnp.exp(jnp.where(inside, differ, 0.0)), 0.0)
    grams = jnp.einsum(
        "...ik,...jk->...ij", jnp.concatenate([keys, query], axis=-2), keys, precision=highest
    )
    keygram = grams[..., :length, :]
    strict = jnp.where(col_ids < row_ids, beta[..., :, None] * keygram * decay_mask, 0.0)
    inverse = unit_lower_inverse(strict, row_ids, col_ids)
    updates = jnp.einsum(
        "...ij,...jd->...id",
        inverse,
        jnp.concatenate([beta[..., None] * values, (beta * jnp.exp(cumul))[..., None] * keys], axis=-1),
        precision=high,
    )
    upd_values = updates[..., : values.shape[-1]]
    upd_keys = updates[..., values.shape[-1] :]
    scores = grams[..., length:, :] * decay_mask
    last_log = cumul[..., -1:]
    query_decay = query * jnp.exp(cumul)[..., None]
    key_decay = keys * jnp.exp(last_log - cumul)[..., None]
    return (upd_values, upd_keys, scores, query_decay, key_decay, last_log[..., 0])


def group_step(state, terms):
    upd_values, upd_keys, scores, query_decay, key_decay, last_log = terms
    new_values = upd_values - jnp.einsum("...ik,...kd->...id", upd_keys, state, precision=highest)
    output = jnp.einsum("...ik,...kd->...id", query_decay, state, precision=highest)
    output = output + jnp.einsum("...ij,...jd->...id", scores, new_values, precision=highest)
    state = jnp.exp(last_log)[..., None, None] * state + jnp.einsum(
        "...ik,...id->...kd", key_decay, new_values, precision=highest
    )
    return (state, output)


def matmul_pair(left_mats, right_mats, precision=high):
    return jnp.einsum("...ij,...jk->...ik", left_mats, right_mats, precision=precision)


def body(
    query_in,
    key_in,
    value_in,
    query_taps,
    key_taps,
    value_taps,
    log_decay,
    beta_logit,
    gate_in,
    norm_gain,
):
    head_size = norm_gain.shape[0]
    length = query_in.shape[0]
    value_heads = log_decay.shape[0]
    key_heads = query_in.shape[1] // head_size
    share_ratio = value_heads // key_heads
    rim_width = query_taps.shape[0] - 1
    groups_dev = length // GROUP
    query_width, key_width = query_in.shape[1], key_in.shape[1]
    tails = shifted(
        jnp.concatenate(
            [query_in[length - rim_width :], key_in[length - rim_width :], value_in[length - rim_width :]],
            axis=1,
        ),
        "ctx",
        1,
    )
    tail_rows = (
        tails[:, :query_width],
        tails[:, query_width : query_width + key_width],
        tails[:, query_width + key_width :],
    )
    query_conv = causal_conv(jnp.concatenate([tail_rows[0], query_in], axis=0), query_taps, length)
    key_conv = causal_conv(jnp.concatenate([tail_rows[1], key_in], axis=0), key_taps, length)
    value_conv = causal_conv(jnp.concatenate([tail_rows[2], value_in], axis=0), value_taps, length)
    queries = (
        unit_rows(query_conv.reshape(length, key_heads, head_size)) * head_size ** (-0.5)
    ).astype(jnp.bfloat16)
    keys = unit_rows(key_conv.reshape(length, key_heads, head_size)).astype(jnp.bfloat16)
    values = value_conv.reshape(length, value_heads, head_size).astype(jnp.bfloat16)

    def blocked(array):
        return (
            array.astype(jnp.float32)
            .reshape(groups_dev, GROUP, array.shape[1], head_size)
            .transpose(0, 2, 1, 3)
        )

    def blocked_rates(array):
        return array.reshape(value_heads, groups_dev, GROUP).transpose(1, 0, 2)

    query_blocks = blocked(jnp.repeat(queries, share_ratio, axis=1))
    key_blocks = blocked(jnp.repeat(keys, share_ratio, axis=1))
    value_blocks = blocked(values)
    beta_blocks = blocked_rates(jax.nn.sigmoid(beta_logit))
    decay_blocks = blocked_rates(log_decay)
    terms = group_terms(query_blocks, key_blocks, value_blocks, beta_blocks, decay_blocks)
    upd_values, upd_keys, scores, query_decay, key_decay, last_log = terms
    identity_state = jnp.broadcast_to(
        jnp.eye(head_size, dtype=jnp.float32), (value_heads, head_size, head_size)
    )
    map_terms = jnp.einsum(
        "...ik,...ij->...kj", key_decay, jnp.concatenate([upd_keys, upd_values], axis=-1), precision=high
    )
    group_maps = jnp.exp(last_log)[..., None, None] * identity_state - map_terms[..., :head_size]
    group_offsets = map_terms[..., head_size:]
    score_terms = matmul_pair(scores, jnp.concatenate([upd_keys, upd_values], axis=-1))
    query_effect = query_decay - score_terms[..., :head_size]
    zero_state = jnp.zeros((value_heads, head_size, head_size), jnp.float32)
    unit_span = jnp.concatenate([identity_state, zero_state], axis=-1)

    def compose(later, earlier):
        product = matmul_pair(later[..., :head_size], earlier)
        return product + jnp.concatenate([jnp.zeros_like(later[..., :head_size]), later[..., head_size:]], axis=-1)

    spans = jnp.concatenate([group_maps, group_offsets], axis=-1)
    reach = 1
    while reach < groups_dev:
        prior = jnp.concatenate(
            [jnp.broadcast_to(unit_span, (reach,) + unit_span.shape), spans[: groups_dev - reach]]
        )
        spans = compose(spans, prior)
        reach *= 2
    shard_map_mat, local_state = spans[-1][..., :head_size], spans[-1][..., head_size:]
    entry_terms = matmul_pair(query_effect, jnp.concatenate([unit_span[None], spans[:-1]]))
    state_effect = entry_terms[..., :head_size]
    local_out = entry_terms[..., head_size:] + score_terms[..., head_size:]

    ctx_count = lax.axis_size("ctx")
    span_map, span_state = shard_map_mat, local_state
    reach = 1
    while reach < ctx_count:
        if 2 * reach < ctx_count:
            prior_map, prior_state = shifted((span_map, span_state), "ctx", reach)
            span_state = matmul_pair(span_map, prior_state) + span_state
            span_map = matmul_pair(span_map, prior_map)
        else:
            prior_state = shifted(span_state, "ctx", reach)
            span_state = matmul_pair(span_map, prior_state) + span_state
        reach *= 2
    incoming = shifted(span_state, "ctx", 1)

    carried_out = jnp.einsum("ghik,hkd->ghid", state_effect, incoming, precision=high)
    output = (local_out + carried_out).transpose(0, 2, 1, 3).reshape(length, value_heads, head_size)
    gates = gate_in.reshape(length, value_heads, head_size).astype(jnp.float32)
    normed = (
        output
        * lax.rsqrt(jnp.mean(output * output, axis=-1, keepdims=True) + norm_eps)
        * norm_gain
        * jax.nn.silu(gates)
    )
    normed = normed.astype(jnp.bfloat16).reshape(length, value_heads * head_size)
    return lax.all_to_all(normed, "head", split_axis=0, concat_axis=1, tiled=True)


def solution(mesh):
    in_specs = (
        P("ctx", "head"),
        P("ctx", "head"),
        P("ctx", "head"),
        P(None, "head"),
        P(None, "head"),
        P(None, "head"),
        P("head", "ctx"),
        P("head", "ctx"),
        P("ctx", "head"),
        P(),
    )
    out_specs = P(("ctx", "head"), None)
    return jax.shard_map(body, mesh=mesh, in_specs=in_specs, out_specs=out_specs, check_vma=False)
```

profile of v0, /device:TPU:4, one launch (start us, length us, event | category | flops | bytes accessed | tf_op | source)
XLA Modules:
  0.0 186.1 jit_solution(3064193533172550019)
XLA Ops:
  2.4 3.8 %collective-permute-start = (bf16[3,1024]{0,1:T(8,128)(2,1)S(1)}, bf16[3,1024]{0,1:T(8,128)(2,1)S(1)}, u32[]{:S(2)}, u32[]{:S(2)}) collective-permute-start(bf16[3,1024]{0,1:T(8,128)(2,1)S(1)} %copy.138), channel_id=1, source_target_pairs={{0,8},{8,16},{16,24},{24,32},{32,40},{40,48},{48,56},{56,64},{64,7... | collective-permute-start | bytes 18440 | tf_op jit(solution)/shard_map/ppermute | solution.py:17
  22.6 2.3 %fusion.46 = f32[8,4,128,64]{2,3,1,0:T(8,128)S(1)} fusion(f32[8,4,64,128]{3,2,1,0:T(8,128)S(1)} %bitcast.111, f32[8,4,64,128]{3,2,1,0:T(8,128)S(1)} %bitcast_convert_fusion, bf16[8,64,4,128]{3,1,0,2:T(8,128)(2,1)S(1)} %bitcast.104), kind=kOutput, calls=%fused_computation.60 | convolution fusion | flops 403177472 | bytes 3670016 | tf_op jit(solution)/shard_map/...ik,...jk->...ij/dot_general | solution.py:56
  28.0 19.7 %while.18 = (s32[]{:T(128)}, f32[8,4,64,64]{3,2,1,0:T(8,128)S(1)}, f32[8,4,64,64]{2,3,1,0:T(8,128)S(1)}, s32[]{:T(128)}, s32[]{:T(128)}) while((s32[]{:T(128)}, f32[8,4,64,64]{3,2,1,0:T(8,128)S(1)}, f32[8,4,64,64]{2,3,1,0:T(8,128)S(1)}, s32[]{:T(128)}, s32[]{:T(128)}) %tuple.74), condition=%wide.region_4.5_spmd.clone.clone, body=%wide.region_3.4_spmd.clone.clone.sunk | while | flops 201723904 | bytes 4202613 | solution.py:45
  28.8 1.8 fusion.148
  32.8 1.8 fusion.148
  36.7 1.8 fusion.148
  40.6 1.8 fusion.148
  44.6 1.8 fusion.148
  47.8 2.5 %fusion.79 = f32[512,512]{1,0:T(8,128)S(1)} fusion(bf16[512,512]{1,0:T(8,128)(2,1)} %param.14, f32[512]{0:T(512)S(1)} %bitcast.122, bf16[3,512]{1,0:T(4,128)(2,1)S(1)} %copy.158, f32[512]{0:T(512)S(1)} %bitcast.123, f32[512]{0:T(512)S(1)} %bitcast.121, f32[512]{0:T(512)S(1)} %bitcast.120), kind=kLoop, calls=%fused_computation.124 | loop fusion | flops 6815744 | bytes 1584128 | tf_op jit(solution)/shard_map/transpose | solution.py:138
  51.6 1.9 %bitcast_multiply_fusion.1 = (f32[8,4,64,128]{3,2,1,0:T(8,128)S(1)}, f32[8,4,64,128]{3,2,1,0:T(8,128)S(1)}) fusion(f32[8,64,4,128]{3,2,1,0:T(4,128)} %reshape.104, f32[8,4,64]{2,1,0:T(4,128)S(1)} %copy.155, bf16[8,64,4,128]{3,1,0,2:T(8,128)(2,1)S(1)} %bitcast.105, f32[8,4,64]{2,1,0:T(4,128)S(1)} %copy-done.13), kind=kLoop, calls=%fused_computation.94 | loop fusion | flops 786432 | bytes 3686400 | tf_op jit(solution)/shard_map/mul | solution.py:65
  55.4 2.4 %fusion.54 = f32[8,4,128,256]{3,2,1,0:T(8,128)S(1)} fusion(f32[8,4,64,128]{3,2,1,0:T(8,128)S(1)} %get-tuple-element.272, f32[8,4,64,128]{3,2,1,0:T(8,128)S(1)} %get-tuple-element.271, f32[8,4,64]{2,1,0:T(4,128)S(1)} %copy-done.12, bf16[8,64,4,128]{3,1,0,2:T(8,128)(2,1)S(1)} %bitcast.106), kind=kOutput, calls=%fused_computation.69 | convolution fusion | flops 403701760 | bytes 6823936 | tf_op jit(solution)/shard_map/...ik,...ij->...kj/dot_general | solution.py:154
  58.9 2.2 %pad_add_fusion.2 = f32[8,4,128,256]{3,2,1,0:T(8,128)S(1)} fusion(f32[8,4,128,128]{3,2,1,0:T(8,128)S(1)} %get-tuple-element.270, f32[8,4,128,128]{3,2,1,0:T(8,128)S(1)} %get-tuple-element.269, f32[1,4,128,256]{3,2,1,0:T(8,128)S(1)} %copy-done.6), kind=kOutput, calls=%fused_computation.56 | convolution fusion | flops 808452096 | bytes 8912896 | tf_op jit(solution)/shard_map/...ij,...jk->...ik/dot_general | solution.py:89
  61.7 2.6 %pad_add_fusion.1 = f32[8,4,128,256]{3,2,1,0:T(8,128)S(1)} fusion(f32[8,4,128,128]{3,2,1,0:T(8,128)S(1)} %slice.222, f32[6,4,128,256]{3,2,1,0:T(8,128)S(1)} %slice.221, f32[2,4,128,256]{3,2,1,0:T(8,128)S(1)} %broadcast_in_dim.83, f32[8,4,128,256]{3,2,1,0:T(8,128)S(1)} %pad_add_fusion.2), kind=kOutput, calls=%fused_computation.55 | convolution fusion | flops 807403520 | bytes 12582912 | tf_op jit(solution)/shard_map/...ij,...jk->...ik/dot_general | solution.py:89
  64.3 2.0 %copy-done.1 = f32[8,4,128,256]{3,2,1,0:T(8,128)} copy-done((f32[8,4,128,256]{3,2,1,0:T(8,128)}, f32[8,4,128,256]{3,2,1,0:T(8,128)S(1)}, u32[]{:S(2)}) %copy-start.1) | copy-done | bytes 4194328
  68.0 4.1 %pad_add_fusion = f32[8,4,128,256]{3,2,1,0:T(8,128)S(1)} fusion(f32[8,4,128,128]{3,2,1,0:T(8,128)S(1)} %slice.225, f32[4,4,128,256]{3,2,1,0:T(8,128)S(1)} %slice-done, f32[4,4,128,256]{3,2,1,0:T(8,128)S(1)} %broadcast_in_dim.84, f32[8,4,128,256]{3,2,1,0:T(8,128)} %copy-done.1), kind=kOutput, calls=%fused_computation.54 | convolution fusion | flops 807403520 | bytes 12582912 | tf_op jit(solution)/shard_map/...ij,...jk->...ik/dot_general | solution.py:89
  72.2 3.8 %collective-permute-start.5 = (f32[4,128,128]{2,1,0:T(8,128)S(1)}, f32[4,128,128]{2,1,0:T(8,128)S(1)}, u32[]{:S(2)}, u32[]{:S(2)}) collective-permute-start(f32[4,128,128]{2,1,0:T(8,128)S(1)} %get-tuple-element.274), channel_id=1, source_target_pairs={{0,8},{8,16},{16,24},{24,32},{32,40},{40,48},{48,56},{56,64},{64,7... | collective-permute-start | bytes 786440 | tf_op jit(solution)/shard_map/ppermute | solution.py:17
  76.1 3.8 %collective-permute-start.1 = (f32[4,128,128]{2,1,0:T(8,128)S(1)}, f32[4,128,128]{2,1,0:T(8,128)S(1)}, u32[]{:S(2)}, u32[]{:S(2)}) collective-permute-start(f32[4,128,128]{2,1,0:T(8,128)S(1)} %get-tuple-element.273), channel_id=1, source_target_pairs={{0,8},{8,16},{16,24},{24,32},{32,40},{40,48},{48,56},{56,64},{64,7... | collective-permute-start | bytes 786440 | tf_op jit(solution)/shard_map/ppermute | solution.py:17
  79.9 5.5 %collective-permute-done.5 = f32[4,128,128]{2,1,0:T(8,128)S(1)} collective-permute-done((f32[4,128,128]{2,1,0:T(8,128)S(1)}, f32[4,128,128]{2,1,0:T(8,128)S(1)}, u32[]{:S(2)}, u32[]{:S(2)}) %collective-permute-start.5) | collective-permute-done | bytes 262176 | tf_op jit(solution)/shard_map/ppermute | solution.py:17
  85.7 3.7 %collective-permute-start.6 = (f32[4,128,128]{2,1,0:T(8,128)S(1)}, f32[4,128,128]{2,1,0:T(8,128)S(1)}, u32[]{:S(2)}, u32[]{:S(2)}) collective-permute-start(f32[4,128,128]{2,1,0:T(8,128)S(1)} %convolution_add_fusion.4), channel_id=1, source_target_pairs={{0,16},{8,24},{16,32},{24,40},{32,48},{40,56},{48,64},{56,72},{64,... | collective-permute-start | bytes 786440 | tf_op jit(solution)/shard_map/ppermute | solution.py:17
  91.3 4.7 %collective-permute-start.2 = (f32[4,128,128]{2,1,0:T(8,128)S(1)}, f32[4,128,128]{2,1,0:T(8,128)S(1)}, u32[]{:S(2)}, u32[]{:S(2)}) collective-permute-start(f32[4,128,128]{2,1,0:T(8,128)S(1)} %fusion.102), channel_id=1, source_target_pairs={{0,16},{8,24},{16,32},{24,40},{32,48},{40,56},{48,64},{56,72},{64,... | collective-permute-start | bytes 786440 | tf_op jit(solution)/shard_map/ppermute | solution.py:17
  96.0 6.6 %collective-permute-done.6 = f32[4,128,128]{2,1,0:T(8,128)S(1)} collective-permute-done((f32[4,128,128]{2,1,0:T(8,128)S(1)}, f32[4,128,128]{2,1,0:T(8,128)S(1)}, u32[]{:S(2)}, u32[]{:S(2)}) %collective-permute-start.6) | collective-permute-done | bytes 262176 | tf_op jit(solution)/shard_map/ppermute | solution.py:17
  102.8 6.9 %collective-permute-start.7 = (f32[4,128,128]{2,1,0:T(8,128)S(1)}, f32[4,128,128]{2,1,0:T(8,128)S(1)}, u32[]{:S(2)}, u32[]{:S(2)}) collective-permute-start(f32[4,128,128]{2,1,0:T(8,128)S(1)} %convolution_add_fusion.3), channel_id=1, source_target_pairs={{0,32},{8,40},{16,48},{24,56},{32,64},{40,72},{48,80},{56,88},{64,... | collective-permute-start | bytes 786440 | tf_op jit(solution)/shard_map/ppermute | solution.py:17
  109.8 6.5 %collective-permute-done.2 = f32[4,128,128]{2,1,0:T(8,128)S(1)} collective-permute-done((f32[4,128,128]{2,1,0:T(8,128)S(1)}, f32[4,128,128]{2,1,0:T(8,128)S(1)}, u32[]{:S(2)}, u32[]{:S(2)}) %collective-permute-start.2) | collective-permute-done | bytes 262176 | tf_op jit(solution)/shard_map/ppermute | solution.py:17
  116.6 13.7 %collective-permute-start.3 = (f32[4,128,128]{2,1,0:T(8,128)S(1)}, f32[4,128,128]{2,1,0:T(8,128)S(1)}, u32[]{:S(2)}, u32[]{:S(2)}) collective-permute-start(f32[4,128,128]{2,1,0:T(8,128)S(1)} %fusion.113), channel_id=1, source_target_pairs={{0,32},{8,40},{16,48},{24,56},{32,64},{40,72},{48,80},{56,88},{64,... | collective-permute-start | bytes 786440 | tf_op jit(solution)/shard_map/ppermute | solution.py:17
  130.5 5.5 %collective-permute-start.8 = (f32[4,128,128]{2,1,0:T(8,128)S(1)}, f32[4,128,128]{2,1,0:T(8,128)S(1)}, u32[]{:S(2)}, u32[]{:S(2)}) collective-permute-start(f32[4,128,128]{2,1,0:T(8,128)S(1)} %convolution_add_fusion.2), channel_id=1, source_target_pairs={{0,64},{8,72},{16,80},{24,88},{32,96},{40,104},{48,112},{56,120},{... | collective-permute-start | bytes 786440 | tf_op jit(solution)/shard_map/ppermute | solution.py:17
  136.1 3.8 %collective-permute-done.3 = f32[4,128,128]{2,1,0:T(8,128)S(1)} collective-permute-done((f32[4,128,128]{2,1,0:T(8,128)S(1)}, f32[4,128,128]{2,1,0:T(8,128)S(1)}, u32[]{:S(2)}, u32[]{:S(2)}) %collective-permute-start.3) | collective-permute-done | bytes 262176 | tf_op jit(solution)/shard_map/ppermute | solution.py:17
  140.1 3.5 %collective-permute-start.4 = (f32[4,128,128]{2,1,0:T(8,128)S(1)}, f32[4,128,128]{2,1,0:T(8,128)S(1)}, u32[]{:S(2)}, u32[]{:S(2)}) collective-permute-start(f32[4,128,128]{2,1,0:T(8,128)S(1)} %fusion.114), channel_id=1, source_target_pairs={{0,64},{8,72},{16,80},{24,88},{32,96},{40,104},{48,112},{56,120},{... | collective-permute-start | bytes 786440 | tf_op jit(solution)/shard_map/ppermute | solution.py:17
  145.3 1.7 fusion.55
  148.7 6.8 %collective-permute-done.9 = f32[4,128,128]{2,1,0:T(8,128)S(1)} collective-permute-done((f32[4,128,128]{2,1,0:T(8,128)S(1)}, f32[4,128,128]{2,1,0:T(8,128)S(1)}, u32[]{:S(2)}, u32[]{:S(2)}) %collective-permute-start.9) | collective-permute-done | bytes 262176 | tf_op jit(solution)/shard_map/ppermute | solution.py:17
  155.8 1.9 %collective-permute-start.10 = (f32[4,128,128]{2,1,0:T(8,128)S(1)}, f32[4,128,128]{2,1,0:T(8,128)S(1)}, u32[]{:S(2)}, u32[]{:S(2)}) collective-permute-start(f32[4,128,128]{2,1,0:T(8,128)S(1)} %convolution_add_fusion), channel_id=1, source_target_pairs={{0,8},{8,16},{16,24},{24,32},{32,40},{40,48},{48,56},{56,64},{64,7... | collective-permute-start | bytes 786440 | tf_op jit(solution)/shard_map/ppermute | solution.py:17
  159.2 7.0 %collective-permute-done.10 = f32[4,128,128]{2,1,0:T(8,128)S(1)} collective-permute-done((f32[4,128,128]{2,1,0:T(8,128)S(1)}, f32[4,128,128]{2,1,0:T(8,128)S(1)}, u32[]{:S(2)}, u32[]{:S(2)}) %collective-permute-start.10) | collective-permute-done | bytes 262176 | tf_op jit(solution)/shard_map/ppermute | solution.py:17
  168.9 16.3 %all_to_all.19 = bf16[8,64,512]{2,1,0:T(8,128)(2,1)S(1)} all-to-all(bf16[8,64,512]{2,1,0:T(8,128)(2,1)S(1)} %bitcast.116), channel_id=1, replica_groups=mesh['ctx'=32,'head'=8] {'head'}, dimensions={0} | all-to-all | bytes 1048576 | tf_op jit(solution)/shard_map/all_to_all | solution.py:205
  (156 shorter events, 50.3 us)
Async XLA Ops:
  0.0 136.1 %copy-start = (f32[128]{0:T(128)S(1)}, f32[128]{0:T(128)}, u32[]{:S(2)}) copy-start(f32[128]{0:T(128)} %param.21) | copy-start | bytes 1540
  0.0 15.6 %copy-start.10 = (bf16[512,256]{1,0:T(8,128)(2,1)S(1)}, bf16[512,256]{1,0:T(8,128)(2,1)}, u32[]{:S(2)}) copy-start(bf16[512,256]{1,0:T(8,128)(2,1)} %param.12) | copy-start | bytes 786436
  0.0 15.4 %copy-start.9 = (bf16[512,256]{1,0:T(8,128)(2,1)S(1)}, bf16[512,256]{1,0:T(8,128)(2,1)}, u32[]{:S(2)}) copy-start(bf16[512,256]{1,0:T(8,128)(2,1)} %param.13) | copy-start | bytes 786436
  2.4 14.6 %collective-permute-start = (bf16[3,1024]{0,1:T(8,128)(2,1)S(1)}, bf16[3,1024]{0,1:T(8,128)(2,1)S(1)}, u32[]{:S(2)}, u32[]{:S(2)}) collective-permute-start(bf16[3,1024]{0,1:T(8,128)(2,1)S(1)} %copy.138), channel_id=1, source_target_pairs={{0,8},{8,16},{16,24},{24,32},{32,40},{40,48},{48,56},{56,64},{64,7... | collective-permute-start | bytes 18440 | tf_op jit(solution)/shard_map/ppermute | solution.py:17
  19.3 0.8 copy-start.11
  21.6 1.0 copy-start.4
  22.6 2.3 %copy-start.15 = (pred[64,64]{0,1:T(8,128)(4,1)S(1)}, pred[64,64]{0,1:T(8,128)(4,1)}, u32[]{:S(2)}) copy-start(pred[64,64]{0,1:T(8,128)(4,1)} %select_compare_fusion) | copy-start | bytes 12292
  22.6 2.3 %copy-start.16 = (pred[64,64]{0,1:T(8,128)(4,1)S(1)}, pred[64,64]{0,1:T(8,128)(4,1)}, u32[]{:S(2)}) copy-start(pred[64,64]{0,1:T(8,128)(4,1)} %get-tuple-element.298) | copy-start | bytes 12292
  24.9 1.5 copy-start.2
  27.9 19.8 %slice-start.1 = ((bf16[3,1024]{0,1:T(8,128)(2,1)}), bf16[3,512]{0,1:T(8,128)(2,1)S(1)}, s32[]{:S(2)}) async-start(bf16[3,1024]{0,1:T(8,128)(2,1)} %copy-done.7), calls=%async_computation.2 | async-start | bytes 262144 | tf_op jit(solution)/shard_map/slice | solution.py:123
  27.9 19.9 %copy-start.17 = (f32[1,512]{1,0:T(1,128)S(1)}, f32[1,512]{1,0:T(1,128)}, u32[]{:S(2)}) copy-start(f32[1,512]{1,0:T(1,128)} %get-tuple-element.282) | copy-start | bytes 6148
  28.0 19.9 %copy-start.18 = (f32[1,512]{1,0:T(1,128)S(1)}, f32[1,512]{1,0:T(1,128)}, u32[]{:S(2)}) copy-start(f32[1,512]{1,0:T(1,128)} %get-tuple-element.283) | copy-start | bytes 6148
  28.0 19.9 %copy-start.19 = (f32[1,512]{1,0:T(1,128)S(1)}, f32[1,512]{1,0:T(1,128)}, u32[]{:S(2)}) copy-start(f32[1,512]{1,0:T(1,128)} %get-tuple-element.284) | copy-start | bytes 6148
  28.0 19.9 %copy-start.20 = (f32[1,512]{1,0:T(1,128)S(1)}, f32[1,512]{1,0:T(1,128)}, u32[]{:S(2)}) copy-start(f32[1,512]{1,0:T(1,128)} %get-tuple-element.285) | copy-start | bytes 6148
  47.7 4.0 %copy-start.13 = (f32[8,4,64]{2,1,0:T(4,128)S(1)}, f32[8,4,64]{2,1,0:T(4,128)}, u32[]{:S(2)}) copy-start(f32[8,4,64]{2,1,0:T(4,128)} %copy.160) | copy-start | bytes 24580
  57.8 1.0 copy-start.6
  64.3 2.0 %copy-start.1 = (f32[8,4,128,256]{3,2,1,0:T(8,128)}, f32[8,4,128,256]{3,2,1,0:T(8,128)S(1)}, u32[]{:S(2)}) copy-start(f32[8,4,128,256]{3,2,1,0:T(8,128)S(1)} %pad_add_fusion.1) | copy-start | bytes 12582916
  66.4 1.6 slice-start
  72.2 13.2 %collective-permute-start.5 = (f32[4,128,128]{2,1,0:T(8,128)S(1)}, f32[4,128,128]{2,1,0:T(8,128)S(1)}, u32[]{:S(2)}, u32[]{:S(2)}) collective-permute-start(f32[4,128,128]{2,1,0:T(8,128)S(1)} %get-tuple-element.274), channel_id=1, source_target_pairs={{0,8},{8,16},{16,24},{24,32},{32,40},{40,48},{48,56},{56,64},{64,7... | collective-permute-start | bytes 786440 | tf_op jit(solution)/shard_map/ppermute | solution.py:17
  76.1 60.0 %copy-start.14 = (f32[8,4,64]{2,0,1:T(8,128)S(1)}, f32[8,4,64]{2,0,1:T(8,128)}, u32[]{:S(2)}) copy-start(f32[8,4,64]{2,0,1:T(8,128)} %get-tuple-element.279) | copy-start | bytes 24580
  76.1 15.0 %collective-permute-start.1 = (f32[4,128,128]{2,1,0:T(8,128)S(1)}, f32[4,128,128]{2,1,0:T(8,128)S(1)}, u32[]{:S(2)}, u32[]{:S(2)}) collective-permute-start(f32[4,128,128]{2,1,0:T(8,128)S(1)} %get-tuple-element.273), channel_id=1, source_target_pairs={{0,8},{8,16},{16,24},{24,32},{32,40},{40,48},{48,56},{56,64},{64,7... | collective-permute-start | bytes 786440 | tf_op jit(solution)/shard_map/ppermute | solution.py:17
  85.7 16.9 %collective-permute-start.6 = (f32[4,128,128]{2,1,0:T(8,128)S(1)}, f32[4,128,128]{2,1,0:T(8,128)S(1)}, u32[]{:S(2)}, u32[]{:S(2)}) collective-permute-start(f32[4,128,128]{2,1,0:T(8,128)S(1)} %convolution_add_fusion.4), channel_id=1, source_target_pairs={{0,16},{8,24},{16,32},{24,40},{32,48},{40,56},{48,64},{56,72},{64,... | collective-permute-start | bytes 786440 | tf_op jit(solution)/shard_map/ppermute | solution.py:17
  91.3 25.0 %collective-permute-start.2 = (f32[4,128,128]{2,1,0:T(8,128)S(1)}, f32[4,128,128]{2,1,0:T(8,128)S(1)}, u32[]{:S(2)}, u32[]{:S(2)}) collective-permute-start(f32[4,128,128]{2,1,0:T(8,128)S(1)} %fusion.102), channel_id=1, source_target_pairs={{0,16},{8,24},{16,32},{24,40},{32,48},{40,56},{48,64},{56,72},{64,... | collective-permute-start | bytes 786440 | tf_op jit(solution)/shard_map/ppermute | solution.py:17
  102.8 42.4 %copy-start.3 = (f32[8,4,128,64]{2,3,1,0:T(8,128)S(1)}, f32[8,4,128,64]{2,3,1,0:T(8,128)}, u32[]{:S(2)}) copy-start(f32[8,4,128,64]{2,3,1,0:T(8,128)} %copy-done.2) | copy-start | bytes 3145732
  102.8 27.4 %collective-permute-start.7 = (f32[4,128,128]{2,1,0:T(8,128)S(1)}, f32[4,128,128]{2,1,0:T(8,128)S(1)}, u32[]{:S(2)}, u32[]{:S(2)}) collective-permute-start(f32[4,128,128]{2,1,0:T(8,128)S(1)} %convolution_add_fusion.3), channel_id=1, source_target_pairs={{0,32},{8,40},{16,48},{24,56},{32,64},{40,72},{48,80},{56,88},{64,... | collective-permute-start | bytes 786440 | tf_op jit(solution)/shard_map/ppermute | solution.py:17
  116.6 23.3 %collective-permute-start.3 = (f32[4,128,128]{2,1,0:T(8,128)S(1)}, f32[4,128,128]{2,1,0:T(8,128)S(1)}, u32[]{:S(2)}, u32[]{:S(2)}) collective-permute-start(f32[4,128,128]{2,1,0:T(8,128)S(1)} %fusion.113), channel_id=1, source_target_pairs={{0,32},{8,40},{16,48},{24,56},{32,64},{40,72},{48,80},{56,88},{64,... | collective-permute-start | bytes 786440 | tf_op jit(solution)/shard_map/ppermute | solution.py:17
  130.5 13.1 %collective-permute-start.8 = (f32[4,128,128]{2,1,0:T(8,128)S(1)}, f32[4,128,128]{2,1,0:T(8,128)S(1)}, u32[]{:S(2)}, u32[]{:S(2)}) collective-permute-start(f32[4,128,128]{2,1,0:T(8,128)S(1)} %convolution_add_fusion.2), channel_id=1, source_target_pairs={{0,64},{8,72},{16,80},{24,88},{32,96},{40,104},{48,112},{56,120},{... | collective-permute-start | bytes 786440 | tf_op jit(solution)/shard_map/ppermute | solution.py:17
  140.1 8.3 %collective-permute-start.4 = (f32[4,128,128]{2,1,0:T(8,128)S(1)}, f32[4,128,128]{2,1,0:T(8,128)S(1)}, u32[]{:S(2)}, u32[]{:S(2)}) collective-permute-start(f32[4,128,128]{2,1,0:T(8,128)S(1)} %fusion.114), channel_id=1, source_target_pairs={{0,64},{8,72},{16,80},{24,88},{32,96},{40,104},{48,112},{56,120},{... | collective-permute-start | bytes 786440 | tf_op jit(solution)/shard_map/ppermute | solution.py:17
  143.9 11.5 %collective-permute-start.9 = (f32[4,128,128]{2,1,0:T(8,128)S(1)}, f32[4,128,128]{2,1,0:T(8,128)S(1)}, u32[]{:S(2)}, u32[]{:S(2)}) collective-permute-start(f32[4,128,128]{2,1,0:T(8,128)S(1)} %convolution_add_fusion.1), channel_id=1, source_target_pairs={{0,128},{8,136},{16,144},{24,152},{32,160},{40,168},{48,176},{56,1... | collective-permute-start | bytes 786440 | tf_op jit(solution)/shard_map/ppermute | solution.py:17
  147.4 10.3 %copy-start.5 = (f32[512,2,2,128]{3,0,2,1:T(8,128)S(1)}, f32[512,2,2,128]{3,0,2,1:T(8,128)}, u32[]{:S(2)}) copy-start(f32[512,2,2,128]{3,0,2,1:T(8,128)} %copy-done.4) | copy-start | bytes 3145732
  155.8 10.4 %collective-permute-start.10 = (f32[4,128,128]{2,1,0:T(8,128)S(1)}, f32[4,128,128]{2,1,0:T(8,128)S(1)}, u32[]{:S(2)}, u32[]{:S(2)}) collective-permute-start(f32[4,128,128]{2,1,0:T(8,128)S(1)} %convolution_add_fusion), channel_id=1, source_target_pairs={{0,8},{8,16},{16,24},{24,32},{32,40},{40,48},{48,56},{56,64},{64,7... | collective-permute-start | bytes 786440 | tf_op jit(solution)/shard_map/ppermute | solution.py:17
  167.1 1.5 copy-start.8
  (6 other events, 4.7 us)
where the time goes:
time: 187 us; the launch traced here: 186 us
  starting transfers between devices  52.7 us (28%)
  waiting for transfers between devices  38.8 us (21%)
  matrix products  36.7 us (20%)
  local copies, waits for them, and re-layouts  24.4 us (13%)
  other arithmetic  16.3 us (9%)
  blocking collectives  16.3 us (9%)
    ppermute x11, starting transfers between devices, shifted(): lax.ppermute(value, axis, [(source, source + steps) for source in range(f...  52.7 us
    ppermute x11, waiting for transfers between devices, shifted(): lax.ppermute(value, axis, [(source, source + steps) for source in range(f...  38.8 us
    dot_general x24, matrix products, matmul_pair(): jnp.einsum('...ij,...jk->...ik', left_mats, right_mats, precision=precision)  29.9 us
    all_to_all x1, blocking collectives, body(): lax.all_to_all(normed, 'head', split_axis=0, concat_axis=1, tiled=True)  16.3 us
    unnamed x54, local copies, waits for them, and re-layouts  6.22 us
    and x5, other arithmetic, level(): (row_ids // (2 * width) == col_ids // (2 * width)) & (row_ids // width !=...  3.74 us
  transfers between devices with their start and end apart: 11, of which 8 were waited for; matrix products, arithmetic and copies ran while one was open for 9% of the time, Pallas kernels for 0%

commit v1 on v0

--- a/solution.py
+++ b/solution.py
@@ -15,6 +15,12 @@
     count = lax.axis_size(axis)
     first, last = (max(0, -steps), min(count, count - steps))
     return lax.ppermute(value, axis, [(source, source + steps) for source in range(first, last)])
+
+
+def shifted_split(value, axis, steps):
+    halves = [(part[: part.shape[0] // 2], part[part.shape[0] // 2 :]) for part in value]
+    moved = shifted(halves, axis, steps)
+    return tuple(jnp.concatenate(pair, axis=0) for pair in moved)
 
 
 def causal_conv(joined, taps, length):
@@ -183,14 +189,14 @@
     reach = 1
     while reach < ctx_count:
         if 2 * reach < ctx_count:
-            prior_map, prior_state = shifted((span_map, span_state), "ctx", reach)
+            prior_map, prior_state = shifted_split((span_map, span_state), "ctx", reach)
             span_state = matmul_pair(span_map, prior_state) + span_state
             span_map = matmul_pair(span_map, prior_map)
         else:
-            prior_state = shifted(span_state, "ctx", reach)
+            (prior_state,) = shifted_split((span_state,), "ctx", reach)
             span_state = matmul_pair(span_map, prior_state) + span_state
         reach *= 2
-    incoming = shifted(span_state, "ctx", 1)
+    (incoming,) = shifted_split((span_state,), "ctx", 1)
 
     carried_out = jnp.einsum("ghik,hkd->ghid", state_effect, incoming, precision=high)
     output = (local_out + carried_out).transpose(0, 2, 1, 3).reshape(length, value_heads, head_size)

time: 187 us -> 199 us (1.064)
  starting transfers between devices: 52.7 us -> 78.9 us
  waiting for transfers between devices: 38.8 us -> 24 us
    ppermute x11 -> x21, starting transfers between devices: 52.7 us -> 78.9 us  [shifted(): lax.ppermute(value, axis, [(source, source + steps) for source in range(f...]
    ppermute x11 -> x21, waiting for transfers between devices: 38.8 us -> 24 us  [shifted(): lax.ppermute(value, axis, [(source, source + steps) for source in range(f...]
    unnamed x54 -> x64, local copies, waits for them, and re-layouts: 6.22 us -> 6.11 us
  transfers between devices with their start and end apart: 11 -> 21, of which waited for: 8 -> 9; matrix products, arithmetic and copies ran while one was open for 9% -> 9% of each run, Pallas kernels for 0% -> 0%
where the time goes in v1:
time: 199 us; the launch traced here: 198 us
  starting transfers between devices  78.9 us (40%)
  matrix products  36.6 us (18%)
  local copies, waits for them, and re-layouts  25.7 us (13%)
  waiting for transfers between devices  24 us (12%)
  other arithmetic  16.5 us (8%)
  blocking collectives  14.7 us (7%)
    ppermute x21, starting transfers between devices, shifted(): lax.ppermute(value, axis, [(source, source + steps) for source in range(f...  78.9 us
    dot_general x24, matrix products, matmul_pair(): jnp.einsum('...ij,...jk->...ik', left_mats, right_mats, precision=precision)  29.9 us
    ppermute x21, waiting for transfers between devices, shifted(): lax.ppermute(value, axis, [(source, source + steps) for source in range(f...  24 us
    all_to_all x1, blocking collectives, body(): lax.all_to_all(normed, 'head', split_axis=0, concat_axis=1, tiled=True)  14.7 us
    unnamed x64, local copies, waits for them, and re-layouts  6.11 us
  transfers between devices with their start and end apart: 21, of which 9 were waited for; matrix products, arithmetic and copies ran while one was open for 9% of the time, Pallas kernels for 0%

profile of v1, /device:TPU:4, one launch (start us, length us, event | category | flops | bytes accessed | tf_op | source)
XLA Modules:
  0.0 197.8 jit_solution(6275116807328875181)
XLA Ops:
  2.4 3.8 %collective-permute-start = (bf16[3,1024]{0,1:T(8,128)(2,1)S(1)}, bf16[3,1024]{0,1:T(8,128)(2,1)S(1)}, u32[]{:S(2)}, u32[]{:S(2)}) collective-permute-start(bf16[3,1024]{0,1:T(8,128)(2,1)S(1)} %copy.138), channel_id=1, source_target_pairs={{0,8},{8,16},{16,24},{24,32},{32,40},{40,48},{48,56},{56,64},{64,7... | collective-permute-start | bytes 18440 | tf_op jit(solution)/shard_map/ppermute | solution.py:17
  24.2 2.3 %fusion.46 = f32[8,4,128,64]{2,3,1,0:T(8,128)S(1)} fusion(f32[8,4,64,128]{3,2,1,0:T(8,128)S(1)} %bitcast.102, f32[8,4,64,128]{3,2,1,0:T(8,128)S(1)} %bitcast_convert_fusion, bf16[8,64,4,128]{3,1,0,2:T(8,128)(2,1)S(1)} %bitcast.95), kind=kOutput, calls=%fused_computation.60 | convolution fusion | flops 403177472 | bytes 3670016 | tf_op jit(solution)/shard_map/...ik,...jk->...ij/dot_general | solution.py:62
  29.7 19.5 %while.18 = (s32[]{:T(128)}, f32[8,4,64,64]{3,2,1,0:T(8,128)S(1)}, f32[8,4,64,64]{2,3,1,0:T(8,128)S(1)}, s32[]{:T(128)}, s32[]{:T(128)}) while((s32[]{:T(128)}, f32[8,4,64,64]{3,2,1,0:T(8,128)S(1)}, f32[8,4,64,64]{2,3,1,0:T(8,128)S(1)}, s32[]{:T(128)}, s32[]{:T(128)}) %tuple.84), condition=%wide.region_4.5_spmd.clone.clone, body=%wide.region_3.4_spmd.clone.clone.sunk | while | flops 201723904 | bytes 4202613 | solution.py:51
  49.3 2.6 %fusion.79 = f32[512,512]{1,0:T(8,128)S(1)} fusion(bf16[512,512]{1,0:T(8,128)(2,1)} %param.14, f32[512]{0:T(512)S(1)} %bitcast.113, bf16[3,512]{1,0:T(4,128)(2,1)S(1)} %copy.158, f32[512]{0:T(512)S(1)} %bitcast.114, f32[512]{0:T(512)S(1)} %bitcast.112, f32[512]{0:T(512)S(1)} %bitcast.111), kind=kLoop, calls=%fused_computation.124 | loop fusion | flops 6815744 | bytes 1584128 | tf_op jit(solution)/shard_map/transpose | solution.py:144
  57.1 2.4 %fusion.54 = f32[8,4,128,256]{3,2,1,0:T(8,128)S(1)} fusion(f32[8,4,64,128]{3,2,1,0:T(8,128)S(1)} %get-tuple-element.272, f32[8,4,64,128]{3,2,1,0:T(8,128)S(1)} %get-tuple-element.271, f32[8,4,64]{2,1,0:T(4,128)S(1)} %copy-done.16, bf16[8,64,4,128]{3,1,0,2:T(8,128)(2,1)S(1)} %bitcast.97), kind=kOutput, calls=%fused_computation.69 | convolution fusion | flops 403701760 | bytes 6823936 | tf_op jit(solution)/shard_map/...ik,...ij->...kj/dot_general | solution.py:160
  60.5 2.2 %pad_add_fusion.2 = f32[8,4,128,256]{3,2,1,0:T(8,128)S(1)} fusion(f32[8,4,128,128]{3,2,1,0:T(8,128)S(1)} %get-tuple-element.270, f32[8,4,128,128]{3,2,1,0:T(8,128)S(1)} %get-tuple-element.269, f32[1,4,128,256]{3,2,1,0:T(8,128)S(1)} %copy-done.8), kind=kOutput, calls=%fused_computation.56 | convolution fusion | flops 808452096 | bytes 8912896 | tf_op jit(solution)/shard_map/...ij,...jk->...ik/dot_general | solution.py:95
  63.3 2.6 %pad_add_fusion.1 = f32[8,4,128,256]{3,2,1,0:T(8,128)S(1)} fusion(f32[8,4,128,128]{3,2,1,0:T(8,128)S(1)} %slice.306, f32[6,4,128,256]{3,2,1,0:T(8,128)S(1)} %slice.305, f32[2,4,128,256]{3,2,1,0:T(8,128)S(1)} %broadcast_in_dim.83, f32[8,4,128,256]{3,2,1,0:T(8,128)S(1)} %pad_add_fusion.2), kind=kOutput, calls=%fused_computation.55 | convolution fusion | flops 807403520 | bytes 12582912 | tf_op jit(solution)/shard_map/...ij,...jk->...ik/dot_general | solution.py:95
  65.9 2.0 %copy-done.2 = f32[8,4,128,256]{3,2,1,0:T(8,128)} copy-done((f32[8,4,128,256]{3,2,1,0:T(8,128)}, f32[8,4,128,256]{3,2,1,0:T(8,128)S(1)}, u32[]{:S(2)}) %copy-start.2) | copy-done | bytes 4194328
  69.6 4.2 %pad_add_fusion = f32[8,4,128,256]{3,2,1,0:T(8,128)S(1)} fusion(f32[8,4,128,128]{3,2,1,0:T(8,128)S(1)} %slice.309, f32[4,4,128,256]{3,2,1,0:T(8,128)S(1)} %slice-done, f32[4,4,128,256]{3,2,1,0:T(8,128)S(1)} %broadcast_in_dim.84, f32[8,4,128,256]{3,2,1,0:T(8,128)} %copy-done.2), kind=kOutput, calls=%fused_computation.54 | convolution fusion | flops 807403520 | bytes 12582912 | tf_op jit(solution)/shard_map/...ij,...jk->...ik/dot_general | solution.py:95
  74.0 4.1 %collective-permute-start.10 = (f32[2,128,128]{2,1,0:T(8,128)S(1)}, f32[2,128,128]{2,1,0:T(8,128)S(1)}, u32[]{:S(2)}, u32[]{:S(2)}) collective-permute-start(f32[2,128,128]{2,1,0:T(8,128)S(1)} %get-tuple-element.274), channel_id=1, source_target_pairs={{0,8},{8,16},{16,24},{24,32},{32,40},{40,48},{48,56},{56,64},{64,7... | collective-permute-start | bytes 393224 | tf_op jit(solution)/shard_map/ppermute | solution.py:17
  78.1 4.0 %collective-permute-start.9 = (f32[2,128,128]{2,1,0:T(8,128)S(1)}, f32[2,128,128]{2,1,0:T(8,128)S(1)}, u32[]{:S(2)}, u32[]{:S(2)}) collective-permute-start(f32[2,128,128]{2,1,0:T(8,128)S(1)} %get-tuple-element.275), channel_id=1, source_target_pairs={{0,8},{8,16},{16,24},{24,32},{32,40},{40,48},{48,56},{56,64},{64,7... | collective-permute-start | bytes 393224 | tf_op jit(solution)/shard_map/ppermute | solution.py:17
  83.9 5.0 %collective-permute-start.1 = (f32[2,128,128]{2,1,0:T(8,128)S(1)}, f32[2,128,128]{2,1,0:T(8,128)S(1)}, u32[]{:S(2)}, u32[]{:S(2)}) collective-permute-start(f32[2,128,128]{2,1,0:T(8,128)S(1)} %get-tuple-element.273), channel_id=1, source_target_pairs={{0,8},{8,16},{16,24},{24,32},{32,40},{40,48},{48,56},{56,64},{64,7... | collective-permute-start | bytes 393224 | tf_op jit(solution)/shard_map/ppermute | solution.py:17
  89.0 2.9 %collective-permute-start.2 = (f32[2,128,128]{2,1,0:T(8,128)S(1)}, f32[2,128,128]{2,1,0:T(8,128)S(1)}, u32[]{:S(2)}, u32[]{:S(2)}) collective-permute-start(f32[2,128,128]{2,1,0:T(8,128)S(1)} %get-tuple-element.276), channel_id=1, source_target_pairs={{0,8},{8,16},{16,24},{24,32},{32,40},{40,48},{48,56},{56,64},{64,7... | collective-permute-start | bytes 393224 | tf_op jit(solution)/shard_map/ppermute | solution.py:17
  92.2 3.4 %collective-permute-start.11 = (f32[2,128,128]{2,1,0:T(8,128)S(1)}, f32[2,128,128]{2,1,0:T(8,128)S(1)}, u32[]{:S(2)}, u32[]{:S(2)}) collective-permute-start(f32[2,128,128]{2,1,0:T(8,128)S(1)} %get-tuple-element.291), channel_id=1, source_target_pairs={{0,16},{8,24},{16,32},{24,40},{32,48},{40,56},{48,64},{56,72},{64,... | collective-permute-start | bytes 393224 | tf_op jit(solution)/shard_map/ppermute | solution.py:17
  95.6 1.9 collective-permute-start.12
  98.4 4.0 %collective-permute-start.3 = (f32[2,128,128]{2,1,0:T(8,128)S(1)}, f32[2,128,128]{2,1,0:T(8,128)S(1)}, u32[]{:S(2)}, u32[]{:S(2)}) collective-permute-start(f32[2,128,128]{2,1,0:T(8,128)S(1)} %get-tuple-element.289), channel_id=1, source_target_pairs={{0,16},{8,24},{16,32},{24,40},{32,48},{40,56},{48,64},{56,72},{64,... | collective-permute-start | bytes 393224 | tf_op jit(solution)/shard_map/ppermute | solution.py:17
  102.4 5.5 %collective-permute-start.4 = (f32[2,128,128]{2,1,0:T(8,128)S(1)}, f32[2,128,128]{2,1,0:T(8,128)S(1)}, u32[]{:S(2)}, u32[]{:S(2)}) collective-permute-start(f32[2,128,128]{2,1,0:T(8,128)S(1)} %get-tuple-element.290), channel_id=1, source_target_pairs={{0,16},{8,24},{16,32},{24,40},{32,48},{40,56},{48,64},{56,72},{64,... | collective-permute-start | bytes 393224 | tf_op jit(solution)/shard_map/ppermute | solution.py:17
  107.9 3.4 %collective-permute-done.12 = f32[2,128,128]{2,1,0:T(8,128)S(1)} collective-permute-done((f32[2,128,128]{2,1,0:T(8,128)S(1)}, f32[2,128,128]{2,1,0:T(8,128)S(1)}, u32[]{:S(2)}, u32[]{:S(2)}) %collective-permute-start.12) | collective-permute-done | bytes 131104 | tf_op jit(solution)/shard_map/ppermute | solution.py:17
  111.6 1.9 collective-permute-start.13
  113.5 8.3 %collective-permute-start.14 = (f32[2,128,128]{2,1,0:T(8,128)S(1)}, f32[2,128,128]{2,1,0:T(8,128)S(1)}, u32[]{:S(2)}, u32[]{:S(2)}) collective-permute-start(f32[2,128,128]{2,1,0:T(8,128)S(1)} %get-tuple-element.288), channel_id=1, source_target_pairs={{0,32},{8,40},{16,48},{24,56},{32,64},{40,72},{48,80},{56,88},{64,... | collective-permute-start | bytes 393224 | tf_op jit(solution)/shard_map/ppermute | solution.py:17
  121.9 3.2 %collective-permute-done.4 = f32[2,128,128]{2,1,0:T(8,128)S(1)} collective-permute-done((f32[2,128,128]{2,1,0:T(8,128)S(1)}, f32[2,128,128]{2,1,0:T(8,128)S(1)}, u32[]{:S(2)}, u32[]{:S(2)}) %collective-permute-start.4) | collective-permute-done | bytes 131104 | tf_op jit(solution)/shard_map/ppermute | solution.py:17
  125.4 1.9 collective-permute-start.5
  127.3 8.0 %collective-permute-start.6 = (f32[2,128,128]{2,1,0:T(8,128)S(1)}, f32[2,128,128]{2,1,0:T(8,128)S(1)}, u32[]{:S(2)}, u32[]{:S(2)}) collective-permute-start(f32[2,128,128]{2,1,0:T(8,128)S(1)} %get-tuple-element.286), channel_id=1, source_target_pairs={{0,32},{8,40},{16,48},{24,56},{32,64},{40,72},{48,80},{56,88},{64,... | collective-permute-start | bytes 393224 | tf_op jit(solution)/shard_map/ppermute | solution.py:17
  135.7 6.0 %collective-permute-start.15 = (f32[2,128,128]{2,1,0:T(8,128)S(1)}, f32[2,128,128]{2,1,0:T(8,128)S(1)}, u32[]{:S(2)}, u32[]{:S(2)}) collective-permute-start(f32[2,128,128]{2,1,0:T(8,128)S(1)} %get-tuple-element.283), channel_id=1, source_target_pairs={{0,64},{8,72},{16,80},{24,88},{32,96},{40,104},{48,112},{56,120},{... | collective-permute-start | bytes 393224 | tf_op jit(solution)/shard_map/ppermute | solution.py:17
  141.7 1.9 collective-permute-start.16
  144.4 7.7 %collective-permute-start.7 = (f32[2,128,128]{2,1,0:T(8,128)S(1)}, f32[2,128,128]{2,1,0:T(8,128)S(1)}, u32[]{:S(2)}, u32[]{:S(2)}) collective-permute-start(f32[2,128,128]{2,1,0:T(8,128)S(1)} %get-tuple-element.281), channel_id=1, source_target_pairs={{0,64},{8,72},{16,80},{24,88},{32,96},{40,104},{48,112},{56,120},{... | collective-permute-start | bytes 393224 | tf_op jit(solution)/shard_map/ppermute | solution.py:17
  157.0 2.0 %collective-permute-done.8 = f32[2,128,128]{2,1,0:T(8,128)S(1)} collective-permute-done((f32[2,128,128]{2,1,0:T(8,128)S(1)}, f32[2,128,128]{2,1,0:T(8,128)S(1)}, u32[]{:S(2)}, u32[]{:S(2)}) %collective-permute-start.8) | collective-permute-done | bytes 131104 | tf_op jit(solution)/shard_map/ppermute | solution.py:17
  159.3 6.5 %collective-permute-done.17 = f32[2,128,128]{2,1,0:T(8,128)S(1)} collective-permute-done((f32[2,128,128]{2,1,0:T(8,128)S(1)}, f32[2,128,128]{2,1,0:T(8,128)S(1)}, u32[]{:S(2)}, u32[]{:S(2)}) %collective-permute-start.17) | collective-permute-done | bytes 131104 | tf_op jit(solution)/shard_map/ppermute | solution.py:17
  165.7 2.4 %collective-permute-done.18 = f32[2,128,128]{2,1,0:T(8,128)S(1)} collective-permute-done((f32[2,128,128]{2,1,0:T(8,128)S(1)}, f32[2,128,128]{2,1,0:T(8,128)S(1)}, u32[]{:S(2)}, u32[]{:S(2)}) %collective-permute-start.18) | collective-permute-done | bytes 131104 | tf_op jit(solution)/shard_map/ppermute | solution.py:17
  173.9 3.6 %collective-permute-done.19 = f32[2,128,128]{2,1,0:T(8,128)S(1)} collective-permute-done((f32[2,128,128]{2,1,0:T(8,128)S(1)}, f32[2,128,128]{2,1,0:T(8,128)S(1)}, u32[]{:S(2)}, u32[]{:S(2)}) %collective-permute-start.19) | collective-permute-done | bytes 131104 | tf_op jit(solution)/shard_map/ppermute | solution.py:17
  177.5 1.9 collective-permute-done.20
  182.2 14.7 %all_to_all.19 = bf16[8,64,512]{2,1,0:T(8,128)(2,1)S(1)} all-to-all(bf16[8,64,512]{2,1,0:T(8,128)(2,1)S(1)} %bitcast.107), channel_id=1, replica_groups=mesh['ctx'=32,'head'=8] {'head'}, dimensions={0} | all-to-all | bytes 1048576 | tf_op jit(solution)/shard_map/all_to_all | solution.py:211
  (194 shorter events, 70.0 us)
Async XLA Ops:
  0.0 14.1 %copy-start = (f32[128]{0:T(128)S(1)}, f32[128]{0:T(128)}, u32[]{:S(2)}) copy-start(f32[128]{0:T(128)} %param.21) | copy-start | bytes 1540
  0.0 16.2 %copy-start.11 = (bf16[512,256]{1,0:T(8,128)(2,1)S(1)}, bf16[512,256]{1,0:T(8,128)(2,1)}, u32[]{:S(2)}) copy-start(bf16[512,256]{1,0:T(8,128)(2,1)} %param.12) | copy-start | bytes 786436
  0.0 16.1 %copy-start.10 = (bf16[512,256]{1,0:T(8,128)(2,1)S(1)}, bf16[512,256]{1,0:T(8,128)(2,1)}, u32[]{:S(2)}) copy-start(bf16[512,256]{1,0:T(8,128)(2,1)} %param.13) | copy-start | bytes 786436
  2.4 17.1 %collective-permute-start = (bf16[3,1024]{0,1:T(8,128)(2,1)S(1)}, bf16[3,1024]{0,1:T(8,128)(2,1)S(1)}, u32[]{:S(2)}, u32[]{:S(2)}) collective-permute-start(bf16[3,1024]{0,1:T(8,128)(2,1)S(1)} %copy.138), channel_id=1, source_target_pairs={{0,8},{8,16},{16,24},{24,32},{32,40},{40,48},{48,56},{56,64},{64,7... | collective-permute-start | bytes 18440 | tf_op jit(solution)/shard_map/ppermute | solution.py:17
  29.6 19.7 %copy-start.21 = (f32[1,512]{1,0:T(1,128)S(1)}, f32[1,512]{1,0:T(1,128)}, u32[]{:S(2)}) copy-start(f32[1,512]{1,0:T(1,128)} %get-tuple-element.300) | copy-start | bytes 6148
  29.6 19.7 %copy-start.22 = (f32[1,512]{1,0:T(1,128)S(1)}, f32[1,512]{1,0:T(1,128)}, u32[]{:S(2)}) copy-start(f32[1,512]{1,0:T(1,128)} %get-tuple-element.301) | copy-start | bytes 6148
  29.6 19.7 %copy-start.23 = (f32[1,512]{1,0:T(1,128)S(1)}, f32[1,512]{1,0:T(1,128)}, u32[]{:S(2)}) copy-start(f32[1,512]{1,0:T(1,128)} %get-tuple-element.302) | copy-start | bytes 6148
  29.6 19.7 %copy-start.24 = (f32[1,512]{1,0:T(1,128)S(1)}, f32[1,512]{1,0:T(1,128)}, u32[]{:S(2)}) copy-start(f32[1,512]{1,0:T(1,128)} %get-tuple-element.303) | copy-start | bytes 6148
  74.0 17.9 %collective-permute-start.10 = (f32[2,128,128]{2,1,0:T(8,128)S(1)}, f32[2,128,128]{2,1,0:T(8,128)S(1)}, u32[]{:S(2)}, u32[]{:S(2)}) collective-permute-start(f32[2,128,128]{2,1,0:T(8,128)S(1)} %get-tuple-element.274), channel_id=1, source_target_pairs={{0,8},{8,16},{16,24},{24,32},{32,40},{40,48},{48,56},{56,64},{64,7... | collective-permute-start | bytes 393224 | tf_op jit(solution)/shard_map/ppermute | solution.py:17
  78.1 13.8 %collective-permute-start.9 = (f32[2,128,128]{2,1,0:T(8,128)S(1)}, f32[2,128,128]{2,1,0:T(8,128)S(1)}, u32[]{:S(2)}, u32[]{:S(2)}) collective-permute-start(f32[2,128,128]{2,1,0:T(8,128)S(1)} %get-tuple-element.275), channel_id=1, source_target_pairs={{0,8},{8,16},{16,24},{24,32},{32,40},{40,48},{48,56},{56,64},{64,7... | collective-permute-start | bytes 393224 | tf_op jit(solution)/shard_map/ppermute | solution.py:17
  83.9 13.6 %collective-permute-start.1 = (f32[2,128,128]{2,1,0:T(8,128)S(1)}, f32[2,128,128]{2,1,0:T(8,128)S(1)}, u32[]{:S(2)}, u32[]{:S(2)}) collective-permute-start(f32[2,128,128]{2,1,0:T(8,128)S(1)} %get-tuple-element.273), channel_id=1, source_target_pairs={{0,8},{8,16},{16,24},{24,32},{32,40},{40,48},{48,56},{56,64},{64,7... | collective-permute-start | bytes 393224 | tf_op jit(solution)/shard_map/ppermute | solution.py:17
  89.0 9.2 %collective-permute-start.2 = (f32[2,128,128]{2,1,0:T(8,128)S(1)}, f32[2,128,128]{2,1,0:T(8,128)S(1)}, u32[]{:S(2)}, u32[]{:S(2)}) collective-permute-start(f32[2,128,128]{2,1,0:T(8,128)S(1)} %get-tuple-element.276), channel_id=1, source_target_pairs={{0,8},{8,16},{16,24},{24,32},{32,40},{40,48},{48,56},{56,64},{64,7... | collective-permute-start | bytes 393224 | tf_op jit(solution)/shard_map/ppermute | solution.py:17
  92.2 15.7 %collective-permute-start.11 = (f32[2,128,128]{2,1,0:T(8,128)S(1)}, f32[2,128,128]{2,1,0:T(8,128)S(1)}, u32[]{:S(2)}, u32[]{:S(2)}) collective-permute-start(f32[2,128,128]{2,1,0:T(8,128)S(1)} %get-tuple-element.291), channel_id=1, source_target_pairs={{0,16},{8,24},{16,32},{24,40},{32,48},{40,56},{48,64},{56,72},{64,... | collective-permute-start | bytes 393224 | tf_op jit(solution)/shard_map/ppermute | solution.py:17
  95.6 15.7 %collective-permute-start.12 = (f32[2,128,128]{2,1,0:T(8,128)S(1)}, f32[2,128,128]{2,1,0:T(8,128)S(1)}, u32[]{:S(2)}, u32[]{:S(2)}) collective-permute-start(f32[2,128,128]{2,1,0:T(8,128)S(1)} %get-tuple-element.292), channel_id=1, source_target_pairs={{0,16},{8,24},{16,32},{24,40},{32,48},{40,56},{48,64},{56,72},{64,... | collective-permute-start | bytes 393224 | tf_op jit(solution)/shard_map/ppermute | solution.py:17
  98.4 23.4 %collective-permute-start.3 = (f32[2,128,128]{2,1,0:T(8,128)S(1)}, f32[2,128,128]{2,1,0:T(8,128)S(1)}, u32[]{:S(2)}, u32[]{:S(2)}) collective-permute-start(f32[2,128,128]{2,1,0:T(8,128)S(1)} %get-tuple-element.289), channel_id=1, source_target_pairs={{0,16},{8,24},{16,32},{24,40},{32,48},{40,56},{48,64},{56,72},{64,... | collective-permute-start | bytes 393224 | tf_op jit(solution)/shard_map/ppermute | solution.py:17
  102.4 22.7 %collective-permute-start.4 = (f32[2,128,128]{2,1,0:T(8,128)S(1)}, f32[2,128,128]{2,1,0:T(8,128)S(1)}, u32[]{:S(2)}, u32[]{:S(2)}) collective-permute-start(f32[2,128,128]{2,1,0:T(8,128)S(1)} %get-tuple-element.290), channel_id=1, source_target_pairs={{0,16},{8,24},{16,32},{24,40},{32,48},{40,56},{48,64},{56,72},{64,... | collective-permute-start | bytes 393224 | tf_op jit(solution)/shard_map/ppermute | solution.py:17
  111.6 23.8 %collective-permute-start.13 = (f32[2,128,128]{2,1,0:T(8,128)S(1)}, f32[2,128,128]{2,1,0:T(8,128)S(1)}, u32[]{:S(2)}, u32[]{:S(2)}) collective-permute-start(f32[2,128,128]{2,1,0:T(8,128)S(1)} %get-tuple-element.287), channel_id=1, source_target_pairs={{0,32},{8,40},{16,48},{24,56},{32,64},{40,72},{48,80},{56,88},{64,... | collective-permute-start | bytes 393224 | tf_op jit(solution)/shard_map/ppermute | solution.py:17
  113.5 21.9 %collective-permute-start.14 = (f32[2,128,128]{2,1,0:T(8,128)S(1)}, f32[2,128,128]{2,1,0:T(8,128)S(1)}, u32[]{:S(2)}, u32[]{:S(2)}) collective-permute-start(f32[2,128,128]{2,1,0:T(8,128)S(1)} %get-tuple-element.288), channel_id=1, source_target_pairs={{0,32},{8,40},{16,48},{24,56},{32,64},{40,72},{48,80},{56,88},{64,... | collective-permute-start | bytes 393224 | tf_op jit(solution)/shard_map/ppermute | solution.py:17
  125.4 18.3 %collective-permute-start.5 = (f32[2,128,128]{2,1,0:T(8,128)S(1)}, f32[2,128,128]{2,1,0:T(8,128)S(1)}, u32[]{:S(2)}, u32[]{:S(2)}) collective-permute-start(f32[2,128,128]{2,1,0:T(8,128)S(1)} %get-tuple-element.285), channel_id=1, source_target_pairs={{0,32},{8,40},{16,48},{24,56},{32,64},{40,72},{48,80},{56,88},{64,... | collective-permute-start | bytes 393224 | tf_op jit(solution)/shard_map/ppermute | solution.py:17
  127.3 16.8 %collective-permute-start.6 = (f32[2,128,128]{2,1,0:T(8,128)S(1)}, f32[2,128,128]{2,1,0:T(8,128)S(1)}, u32[]{:S(2)}, u32[]{:S(2)}) collective-permute-start(f32[2,128,128]{2,1,0:T(8,128)S(1)} %get-tuple-element.286), channel_id=1, source_target_pairs={{0,32},{8,40},{16,48},{24,56},{32,64},{40,72},{48,80},{56,88},{64,... | collective-permute-start | bytes 393224 | tf_op jit(solution)/shard_map/ppermute | solution.py:17
  135.7 18.4 %collective-permute-start.15 = (f32[2,128,128]{2,1,0:T(8,128)S(1)}, f32[2,128,128]{2,1,0:T(8,128)S(1)}, u32[]{:S(2)}, u32[]{:S(2)}) collective-permute-start(f32[2,128,128]{2,1,0:T(8,128)S(1)} %get-tuple-element.283), channel_id=1, source_target_pairs={{0,64},{8,72},{16,80},{24,88},{32,96},{40,104},{48,112},{56,120},{... | collective-permute-start | bytes 393224 | tf_op jit(solution)/shard_map/ppermute | solution.py:17
  141.7 12.3 %collective-permute-start.16 = (f32[2,128,128]{2,1,0:T(8,128)S(1)}, f32[2,128,128]{2,1,0:T(8,128)S(1)}, u32[]{:S(2)}, u32[]{:S(2)}) collective-permute-start(f32[2,128,128]{2,1,0:T(8,128)S(1)} %get-tuple-element.284), channel_id=1, source_target_pairs={{0,64},{8,72},{16,80},{24,88},{32,96},{40,104},{48,112},{56,120},{... | collective-permute-start | bytes 393224 | tf_op jit(solution)/shard_map/ppermute | solution.py:17
  144.1 28.2 %copy-start.7 = (f32[512,2,2,128]{3,0,2,1:T(8,128)S(1)}, f32[512,2,2,128]{3,0,2,1:T(8,128)}, u32[]{:S(2)}) copy-start(f32[512,2,2,128]{3,0,2,1:T(8,128)} %copy-done.6) | copy-start | bytes 3145732
  144.4 28.0 %slice-start.1 = ((f32[8,4,128,256]{3,2,1,0:T(8,128)}), f32[7,4,128,256]{3,2,1,0:T(8,128)S(1)}, s32[]{:S(2)}) async-start(f32[8,4,128,256]{3,2,1,0:T(8,128)} %copy-done.3), calls=%async_computation.2 | async-start | bytes 7340032 | tf_op jit(solution)/shard_map/slice | solution.py:183
  144.4 28.0 %copy-start.15 = (f32[8,4,64]{2,1,0:T(4,128)S(1)}, f32[8,4,64]{2,1,0:T(4,128)}, u32[]{:S(2)}) copy-start(f32[8,4,64]{2,1,0:T(4,128)} %copy.145) | copy-start | bytes 24580
  144.4 12.6 %collective-permute-start.7 = (f32[2,128,128]{2,1,0:T(8,128)S(1)}, f32[2,128,128]{2,1,0:T(8,128)S(1)}, u32[]{:S(2)}, u32[]{:S(2)}) collective-permute-start(f32[2,128,128]{2,1,0:T(8,128)S(1)} %get-tuple-element.281), channel_id=1, source_target_pairs={{0,64},{8,72},{16,80},{24,88},{32,96},{40,104},{48,112},{56,120},{... | collective-permute-start | bytes 393224 | tf_op jit(solution)/shard_map/ppermute | solution.py:17
  152.1 6.9 %collective-permute-start.8 = (f32[2,128,128]{2,1,0:T(8,128)S(1)}, f32[2,128,128]{2,1,0:T(8,128)S(1)}, u32[]{:S(2)}, u32[]{:S(2)}) collective-permute-start(f32[2,128,128]{2,1,0:T(8,128)S(1)} %get-tuple-element.282), channel_id=1, source_target_pairs={{0,64},{8,72},{16,80},{24,88},{32,96},{40,104},{48,112},{56,120},{... | collective-permute-start | bytes 393224 | tf_op jit(solution)/shard_map/ppermute | solution.py:17
  154.4 11.4 %collective-permute-start.17 = (f32[2,128,128]{2,1,0:T(8,128)S(1)}, f32[2,128,128]{2,1,0:T(8,128)S(1)}, u32[]{:S(2)}, u32[]{:S(2)}) collective-permute-start(f32[2,128,128]{2,1,0:T(8,128)S(1)} %get-tuple-element.279), channel_id=1, source_target_pairs={{0,128},{8,136},{16,144},{24,152},{32,160},{40,168},{48,176},{56,1... | collective-permute-start | bytes 393224 | tf_op jit(solution)/shard_map/ppermute | solution.py:17
  155.7 12.5 %collective-permute-start.18 = (f32[2,128,128]{2,1,0:T(8,128)S(1)}, f32[2,128,128]{2,1,0:T(8,128)S(1)}, u32[]{:S(2)}, u32[]{:S(2)}) collective-permute-start(f32[2,128,128]{2,1,0:T(8,128)S(1)} %get-tuple-element.280), channel_id=1, source_target_pairs={{0,128},{8,136},{16,144},{24,152},{32,160},{40,168},{48,176},{56,1... | collective-permute-start | bytes 393224 | tf_op jit(solution)/shard_map/ppermute | solution.py:17
  168.5 9.0 %collective-permute-start.19 = (f32[2,128,128]{2,1,0:T(8,128)S(1)}, f32[2,128,128]{2,1,0:T(8,128)S(1)}, u32[]{:S(2)}, u32[]{:S(2)}) collective-permute-start(f32[2,128,128]{2,1,0:T(8,128)S(1)} %get-tuple-element.277), channel_id=1, source_target_pairs={{0,8},{8,16},{16,24},{24,32},{32,40},{40,48},{48,56},{56,64},{64,7... | collective-permute-start | bytes 393224 | tf_op jit(solution)/shard_map/ppermute | solution.py:17
  170.4 9.0 %collective-permute-start.20 = (f32[2,128,128]{2,1,0:T(8,128)S(1)}, f32[2,128,128]{2,1,0:T(8,128)S(1)}, u32[]{:S(2)}, u32[]{:S(2)}) collective-permute-start(f32[2,128,128]{2,1,0:T(8,128)S(1)} %get-tuple-element.278), channel_id=1, source_target_pairs={{0,8},{8,16},{16,24},{24,32},{32,40},{40,48},{48,56},{56,64},{64,7... | collective-permute-start | bytes 393224 | tf_op jit(solution)/shard_map/ppermute | solution.py:17
  181.8 16.0 %copy-start.1 = (f32[128]{0:T(128)S(1)}, f32[128]{0:T(128)}, u32[]{:S(2)}) copy-start(f32[128]{0:T(128)} %param.21) | copy-start | bytes 1540
  (21 other events, 50.0 us)

commit v2 on v0

--- a/solution.py
+++ b/solution.py
@@ -184,8 +184,9 @@
     while reach < ctx_count:
         if 2 * reach < ctx_count:
             prior_map, prior_state = shifted((span_map, span_state), "ctx", reach)
-            span_state = matmul_pair(span_map, prior_state) + span_state
-            span_map = matmul_pair(span_map, prior_map)
+            joined = matmul_pair(span_map, jnp.concatenate([prior_map, prior_state], axis=-1))
+            span_state = joined[..., head_size:] + span_state
+            span_map = joined[..., :head_size]
         else:
             prior_state = shifted(span_state, "ctx", reach)
             span_state = matmul_pair(span_map, prior_state) + span_state

time: 187 us -> 207 us (1.11)
  waiting for transfers between devices: 38.8 us -> 72.9 us
  starting transfers between devices: 52.7 us -> 40.7 us
    ppermute x11, waiting for transfers between devices: 38.8 us -> 72.9 us  [shifted(): lax.ppermute(value, axis, [(source, source + steps) for source in range(f...]
    ppermute x11, starting transfers between devices: 52.7 us -> 40.7 us  [shifted(): lax.ppermute(value, axis, [(source, source + steps) for source in range(f...]
    dot_general x24 -> x20, matrix products: 29.9 us -> 29.3 us  [matmul_pair(): jnp.einsum('...ij,...jk->...ik', left_mats, right_mats, precision=precision)]
    unnamed x54 -> x56, local copies, waits for them, and re-layouts: 6.22 us -> 6.21 us
  transfers between devices with their start and end apart: 11 -> 11, of which waited for: 8 -> 10; matrix products, arithmetic and copies ran while one was open for 9% -> 7% of each run, Pallas kernels for 0% -> 0%
where the time goes in v2:
time: 207 us; the launch traced here: 206 us
  waiting for transfers between devices  72.9 us (35%)
  starting transfers between devices  40.7 us (20%)
  matrix products  36 us (17%)
  local copies, waits for them, and re-layouts  24 us (12%)
  other arithmetic  16.5 us (8%)
  blocking collectives  14.6 us (7%)
    ppermute x11, waiting for transfers between devices, shifted(): lax.ppermute(value, axis, [(source, source + steps) for source in range(f...  72.9 us
    ppermute x11, starting transfers between devices, shifted(): lax.ppermute(value, axis, [(source, source + steps) for source in range(f...  40.7 us
    dot_general x20, matrix products, matmul_pair(): jnp.einsum('...ij,...jk->...ik', left_mats, right_mats, precision=precision)  29.3 us
    all_to_all x1, blocking collectives, body(): lax.all_to_all(normed, 'head', split_axis=0, concat_axis=1, tiled=True)  14.6 us
    unnamed x56, local copies, waits for them, and re-layouts  6.21 us
  transfers between devices with their start and end apart: 11, of which 10 were waited for; matrix products, arithmetic and copies ran while one was open for 7% of the time, Pallas kernels for 0%

profile of v2, /device:TPU:4, one launch (start us, length us, event | category | flops | bytes accessed | tf_op | source)
XLA Modules:
  0.0 205.7 jit_solution(16025863295309048976)
XLA Ops:
  2.4 3.8 %collective-permute-start = (bf16[3,1024]{0,1:T(8,128)(2,1)S(1)}, bf16[3,1024]{0,1:T(8,128)(2,1)S(1)}, u32[]{:S(2)}, u32[]{:S(2)}) collective-permute-start(bf16[3,1024]{0,1:T(8,128)(2,1)S(1)} %copy.138), channel_id=1, source_target_pairs={{0,8},{8,16},{16,24},{24,32},{32,40},{40,48},{48,56},{56,64},{64,7... | collective-permute-start | bytes 18440 | tf_op jit(solution)/shard_map/ppermute | solution.py:17
  22.6 2.3 %fusion.46 = f32[8,4,128,64]{2,3,1,0:T(8,128)S(1)} fusion(f32[8,4,64,128]{3,2,1,0:T(8,128)S(1)} %bitcast.96, f32[8,4,64,128]{3,2,1,0:T(8,128)S(1)} %bitcast_convert_fusion, bf16[8,64,4,128]{3,1,0,2:T(8,128)(2,1)S(1)} %bitcast.89), kind=kOutput, calls=%fused_computation.60 | convolution fusion | flops 403177472 | bytes 3670016 | tf_op jit(solution)/shard_map/...ik,...jk->...ij/dot_general | solution.py:56
  28.0 19.7 %while.18 = (s32[]{:T(128)}, f32[8,4,64,64]{3,2,1,0:T(8,128)S(1)}, f32[8,4,64,64]{2,3,1,0:T(8,128)S(1)}, s32[]{:T(128)}, s32[]{:T(128)}) while((s32[]{:T(128)}, f32[8,4,64,64]{3,2,1,0:T(8,128)S(1)}, f32[8,4,64,64]{2,3,1,0:T(8,128)S(1)}, s32[]{:T(128)}, s32[]{:T(128)}) %tuple.77), condition=%wide.region_4.5_spmd.clone.clone, body=%wide.region_3.4_spmd.clone.clone.sunk | while | flops 201723904 | bytes 4202613 | solution.py:45
  32.8 1.8 fusion.155
  36.7 1.8 fusion.155
  47.8 2.5 %fusion.95 = f32[512,512]{1,0:T(8,128)S(1)} fusion(bf16[512,512]{1,0:T(8,128)(2,1)} %param.14, f32[512]{0:T(512)S(1)} %bitcast.107, bf16[3,512]{1,0:T(4,128)(2,1)S(1)} %copy.158, f32[512]{0:T(512)S(1)} %bitcast.108, f32[512]{0:T(512)S(1)} %bitcast.106, f32[512]{0:T(512)S(1)} %bitcast.105), kind=kLoop, calls=%fused_computation.136 | loop fusion | flops 6815744 | bytes 1584128 | tf_op jit(solution)/shard_map/transpose | solution.py:138
  51.7 1.9 bitcast_multiply_fusion.1
  55.5 2.4 %fusion.54 = f32[8,4,128,256]{3,2,1,0:T(8,128)S(1)} fusion(f32[8,4,64,128]{3,2,1,0:T(8,128)S(1)} %get-tuple-element.272, f32[8,4,64,128]{3,2,1,0:T(8,128)S(1)} %get-tuple-element.271, f32[8,4,64]{2,1,0:T(4,128)S(1)} %copy-done.13, bf16[8,64,4,128]{3,1,0,2:T(8,128)(2,1)S(1)} %bitcast.91), kind=kOutput, calls=%fused_computation.69 | convolution fusion | flops 403701760 | bytes 6823936 | tf_op jit(solution)/shard_map/...ik,...ij->...kj/dot_general | solution.py:154
  58.9 2.2 %pad_add_fusion.2 = f32[8,4,128,256]{3,2,1,0:T(8,128)S(1)} fusion(f32[8,4,128,128]{3,2,1,0:T(8,128)S(1)} %get-tuple-element.270, f32[8,4,128,128]{3,2,1,0:T(8,128)S(1)} %get-tuple-element.269, f32[1,4,128,256]{3,2,1,0:T(8,128)S(1)} %copy-done.7), kind=kOutput, calls=%fused_computation.56 | convolution fusion | flops 808452096 | bytes 8912896 | tf_op jit(solution)/shard_map/...ij,...jk->...ik/dot_general | solution.py:89
  61.7 2.6 %pad_add_fusion.1 = f32[8,4,128,256]{3,2,1,0:T(8,128)S(1)} fusion(f32[8,4,128,128]{3,2,1,0:T(8,128)S(1)} %slice.254, f32[6,4,128,256]{3,2,1,0:T(8,128)S(1)} %slice.253, f32[2,4,128,256]{3,2,1,0:T(8,128)S(1)} %broadcast_in_dim.83, f32[8,4,128,256]{3,2,1,0:T(8,128)S(1)} %pad_add_fusion.2), kind=kOutput, calls=%fused_computation.55 | convolution fusion | flops 807403520 | bytes 12582912 | tf_op jit(solution)/shard_map/...ij,...jk->...ik/dot_general | solution.py:89
  64.3 2.0 copy-done.1
  68.0 4.1 %pad_add_fusion = f32[8,4,128,256]{3,2,1,0:T(8,128)S(1)} fusion(f32[8,4,128,128]{3,2,1,0:T(8,128)S(1)} %slice.257, f32[4,4,128,256]{3,2,1,0:T(8,128)S(1)} %slice-done, f32[4,4,128,256]{3,2,1,0:T(8,128)S(1)} %broadcast_in_dim.84, f32[8,4,128,256]{3,2,1,0:T(8,128)} %copy-done.1), kind=kOutput, calls=%fused_computation.54 | convolution fusion | flops 807403520 | bytes 12582912 | tf_op jit(solution)/shard_map/...ij,...jk->...ik/dot_general | solution.py:89
  72.3 3.8 %collective-permute-start.1 = (f32[4,128,128]{2,1,0:T(8,128)S(1)}, f32[4,128,128]{2,1,0:T(8,128)S(1)}, u32[]{:S(2)}, u32[]{:S(2)}) collective-permute-start(f32[4,128,128]{2,1,0:T(8,128)S(1)} %get-tuple-element.279), channel_id=1, source_target_pairs={{0,8},{8,16},{16,24},{24,32},{32,40},{40,48},{48,56},{56,64},{64,7... | collective-permute-start | bytes 786440 | tf_op jit(solution)/shard_map/ppermute | solution.py:17
  76.1 3.8 %collective-permute-start.2 = (f32[4,128,128]{2,1,0:T(8,128)S(1)}, f32[4,128,128]{2,1,0:T(8,128)S(1)}, u32[]{:S(2)}, u32[]{:S(2)}) collective-permute-start(f32[4,128,128]{2,1,0:T(8,128)S(1)} %get-tuple-element.280), channel_id=1, source_target_pairs={{0,8},{8,16},{16,24},{24,32},{32,40},{40,48},{48,56},{56,64},{64,7... | collective-permute-start | bytes 786440 | tf_op jit(solution)/shard_map/ppermute | solution.py:17
  79.9 5.5 %collective-permute-done.1 = f32[4,128,128]{2,1,0:T(8,128)S(1)} collective-permute-done((f32[4,128,128]{2,1,0:T(8,128)S(1)}, f32[4,128,128]{2,1,0:T(8,128)S(1)}, u32[]{:S(2)}, u32[]{:S(2)}) %collective-permute-start.1) | collective-permute-done | bytes 262176 | tf_op jit(solution)/shard_map/ppermute | solution.py:17
  85.5 4.6 %collective-permute-done.2 = f32[4,128,128]{2,1,0:T(8,128)S(1)} collective-permute-done((f32[4,128,128]{2,1,0:T(8,128)S(1)}, f32[4,128,128]{2,1,0:T(8,128)S(1)}, u32[]{:S(2)}, u32[]{:S(2)}) %collective-permute-start.2) | collective-permute-done | bytes 262176 | tf_op jit(solution)/shard_map/ppermute | solution.py:17
  90.5 3.4 %collective-permute-start.3 = (f32[4,128,128]{2,1,0:T(8,128)S(1)}, f32[4,128,128]{2,1,0:T(8,128)S(1)}, u32[]{:S(2)}, u32[]{:S(2)}) collective-permute-start(f32[4,128,128]{2,1,0:T(8,128)S(1)} %get-tuple-element.277), channel_id=1, source_target_pairs={{0,16},{8,24},{16,32},{24,40},{32,48},{40,56},{48,64},{56,72},{64,... | collective-permute-start | bytes 786440 | tf_op jit(solution)/shard_map/ppermute | solution.py:17
  93.8 6.3 %collective-permute-start.4 = (f32[4,128,128]{2,1,0:T(8,128)S(1)}, f32[4,128,128]{2,1,0:T(8,128)S(1)}, u32[]{:S(2)}, u32[]{:S(2)}) collective-permute-start(f32[4,128,128]{2,1,0:T(8,128)S(1)} %get-tuple-element.278), channel_id=1, source_target_pairs={{0,16},{8,24},{16,32},{24,40},{32,48},{40,56},{48,64},{56,72},{64,... | collective-permute-start | bytes 786440 | tf_op jit(solution)/shard_map/ppermute | solution.py:17
  100.1 14.6 %collective-permute-done.3 = f32[4,128,128]{2,1,0:T(8,128)S(1)} collective-permute-done((f32[4,128,128]{2,1,0:T(8,128)S(1)}, f32[4,128,128]{2,1,0:T(8,128)S(1)}, u32[]{:S(2)}, u32[]{:S(2)}) %collective-permute-start.3) | collective-permute-done | bytes 262176 | tf_op jit(solution)/shard_map/ppermute | solution.py:17
  114.7 3.9 %collective-permute-done.4 = f32[4,128,128]{2,1,0:T(8,128)S(1)} collective-permute-done((f32[4,128,128]{2,1,0:T(8,128)S(1)}, f32[4,128,128]{2,1,0:T(8,128)S(1)}, u32[]{:S(2)}, u32[]{:S(2)}) %collective-permute-start.4) | collective-permute-done | bytes 262176 | tf_op jit(solution)/shard_map/ppermute | solution.py:17
  119.0 6.0 %collective-permute-start.5 = (f32[4,128,128]{2,1,0:T(8,128)S(1)}, f32[4,128,128]{2,1,0:T(8,128)S(1)}, u32[]{:S(2)}, u32[]{:S(2)}) collective-permute-start(f32[4,128,128]{2,1,0:T(8,128)S(1)} %get-tuple-element.275), channel_id=1, source_target_pairs={{0,32},{8,40},{16,48},{24,56},{32,64},{40,72},{48,80},{56,88},{64,... | collective-permute-start | bytes 786440 | tf_op jit(solution)/shard_map/ppermute | solution.py:17
  125.0 4.9 %collective-permute-start.6 = (f32[4,128,128]{2,1,0:T(8,128)S(1)}, f32[4,128,128]{2,1,0:T(8,128)S(1)}, u32[]{:S(2)}, u32[]{:S(2)}) collective-permute-start(f32[4,128,128]{2,1,0:T(8,128)S(1)} %get-tuple-element.276), channel_id=1, source_target_pairs={{0,32},{8,40},{16,48},{24,56},{32,64},{40,72},{48,80},{56,88},{64,... | collective-permute-start | bytes 786440 | tf_op jit(solution)/shard_map/ppermute | solution.py:17
  129.9 13.8 %collective-permute-done.5 = f32[4,128,128]{2,1,0:T(8,128)S(1)} collective-permute-done((f32[4,128,128]{2,1,0:T(8,128)S(1)}, f32[4,128,128]{2,1,0:T(8,128)S(1)}, u32[]{:S(2)}, u32[]{:S(2)}) %collective-permute-start.5) | collective-permute-done | bytes 262176 | tf_op jit(solution)/shard_map/ppermute | solution.py:17
  143.7 5.5 %collective-permute-done.6 = f32[4,128,128]{2,1,0:T(8,128)S(1)} collective-permute-done((f32[4,128,128]{2,1,0:T(8,128)S(1)}, f32[4,128,128]{2,1,0:T(8,128)S(1)}, u32[]{:S(2)}, u32[]{:S(2)}) %collective-permute-start.6) | collective-permute-done | bytes 262176 | tf_op jit(solution)/shard_map/ppermute | solution.py:17
  149.6 3.3 %collective-permute-start.7 = (f32[4,128,128]{2,1,0:T(8,128)S(1)}, f32[4,128,128]{2,1,0:T(8,128)S(1)}, u32[]{:S(2)}, u32[]{:S(2)}) collective-permute-start(f32[4,128,128]{2,1,0:T(8,128)S(1)} %get-tuple-element.273), channel_id=1, source_target_pairs={{0,64},{8,72},{16,80},{24,88},{32,96},{40,104},{48,112},{56,120},{... | collective-permute-start | bytes 786440 | tf_op jit(solution)/shard_map/ppermute | solution.py:17
  152.9 1.9 collective-permute-start.8
  154.9 5.8 %collective-permute-done.7 = f32[4,128,128]{2,1,0:T(8,128)S(1)} collective-permute-done((f32[4,128,128]{2,1,0:T(8,128)S(1)}, f32[4,128,128]{2,1,0:T(8,128)S(1)}, u32[]{:S(2)}, u32[]{:S(2)}) %collective-permute-start.7) | collective-permute-done | bytes 262176 | tf_op jit(solution)/shard_map/ppermute | solution.py:17
  160.7 4.6 %collective-permute-done.8 = f32[4,128,128]{2,1,0:T(8,128)S(1)} collective-permute-done((f32[4,128,128]{2,1,0:T(8,128)S(1)}, f32[4,128,128]{2,1,0:T(8,128)S(1)}, u32[]{:S(2)}, u32[]{:S(2)}) %collective-permute-start.8) | collective-permute-done | bytes 262176 | tf_op jit(solution)/shard_map/ppermute | solution.py:17
  169.1 7.7 %collective-permute-done.9 = f32[4,128,128]{2,1,0:T(8,128)S(1)} collective-permute-done((f32[4,128,128]{2,1,0:T(8,128)S(1)}, f32[4,128,128]{2,1,0:T(8,128)S(1)}, u32[]{:S(2)}, u32[]{:S(2)}) %collective-permute-start.9) | collective-permute-done | bytes 262176 | tf_op jit(solution)/shard_map/ppermute | solution.py:17
  177.0 1.9 collective-permute-start.10
  180.4 7.1 %collective-permute-done.10 = f32[4,128,128]{2,1,0:T(8,128)S(1)} collective-permute-done((f32[4,128,128]{2,1,0:T(8,128)S(1)}, f32[4,128,128]{2,1,0:T(8,128)S(1)}, u32[]{:S(2)}, u32[]{:S(2)}) %collective-permute-start.10) | collective-permute-done | bytes 262176 | tf_op jit(solution)/shard_map/ppermute | solution.py:17
  190.3 14.6 %all_to_all.19 = bf16[8,64,512]{2,1,0:T(8,128)(2,1)S(1)} all-to-all(bf16[8,64,512]{2,1,0:T(8,128)(2,1)S(1)} %bitcast.101), channel_id=1, replica_groups=mesh['ctx'=32,'head'=8] {'head'}, dimensions={0} | all-to-all | bytes 1048576 | tf_op jit(solution)/shard_map/all_to_all | solution.py:206
  (159 shorter events, 54.4 us)
Async XLA Ops:
  0.0 154.9 %copy-start = (f32[128]{0:T(128)S(1)}, f32[128]{0:T(128)}, u32[]{:S(2)}) copy-start(f32[128]{0:T(128)} %param.21) | copy-start | bytes 1540
  0.0 15.6 %copy-start.11 = (bf16[512,256]{1,0:T(8,128)(2,1)S(1)}, bf16[512,256]{1,0:T(8,128)(2,1)}, u32[]{:S(2)}) copy-start(bf16[512,256]{1,0:T(8,128)(2,1)} %param.12) | copy-start | bytes 786436
  0.0 15.4 %copy-start.10 = (bf16[512,256]{1,0:T(8,128)(2,1)S(1)}, bf16[512,256]{1,0:T(8,128)(2,1)}, u32[]{:S(2)}) copy-start(bf16[512,256]{1,0:T(8,128)(2,1)} %param.13) | copy-start | bytes 786436
  2.4 14.6 %collective-permute-start = (bf16[3,1024]{0,1:T(8,128)(2,1)S(1)}, bf16[3,1024]{0,1:T(8,128)(2,1)S(1)}, u32[]{:S(2)}, u32[]{:S(2)}) collective-permute-start(bf16[3,1024]{0,1:T(8,128)(2,1)S(1)} %copy.138), channel_id=1, source_target_pairs={{0,8},{8,16},{16,24},{24,32},{32,40},{40,48},{48,56},{56,64},{64,7... | collective-permute-start | bytes 18440 | tf_op jit(solution)/shard_map/ppermute | solution.py:17
  22.6 2.3 %copy-start.16 = (pred[64,64]{0,1:T(8,128)(4,1)S(1)}, pred[64,64]{0,1:T(8,128)(4,1)}, u32[]{:S(2)}) copy-start(pred[64,64]{0,1:T(8,128)(4,1)} %select_compare_fusion) | copy-start | bytes 12292
  22.6 2.3 %copy-start.17 = (pred[64,64]{0,1:T(8,128)(4,1)S(1)}, pred[64,64]{0,1:T(8,128)(4,1)}, u32[]{:S(2)}) copy-start(pred[64,64]{0,1:T(8,128)(4,1)} %get-tuple-element.304) | copy-start | bytes 12292
  24.9 1.5 copy-start.3
  27.9 19.8 %slice-start.2 = ((bf16[3,1024]{0,1:T(8,128)(2,1)}), bf16[3,512]{0,1:T(8,128)(2,1)S(1)}, s32[]{:S(2)}) async-start(bf16[3,1024]{0,1:T(8,128)(2,1)} %copy-done.8), calls=%async_computation.3 | async-start | bytes 262144 | tf_op jit(solution)/shard_map/slice | solution.py:123
  28.0 19.9 %copy-start.18 = (f32[1,512]{1,0:T(1,128)S(1)}, f32[1,512]{1,0:T(1,128)}, u32[]{:S(2)}) copy-start(f32[1,512]{1,0:T(1,128)} %get-tuple-element.288) | copy-start | bytes 6148
  28.0 19.9 %copy-start.19 = (f32[1,512]{1,0:T(1,128)S(1)}, f32[1,512]{1,0:T(1,128)}, u32[]{:S(2)}) copy-start(f32[1,512]{1,0:T(1,128)} %get-tuple-element.289) | copy-start | bytes 6148
  28.0 19.9 %copy-start.20 = (f32[1,512]{1,0:T(1,128)S(1)}, f32[1,512]{1,0:T(1,128)}, u32[]{:S(2)}) copy-start(f32[1,512]{1,0:T(1,128)} %get-tuple-element.290) | copy-start | bytes 6148
  28.0 19.9 %copy-start.21 = (f32[1,512]{1,0:T(1,128)S(1)}, f32[1,512]{1,0:T(1,128)}, u32[]{:S(2)}) copy-start(f32[1,512]{1,0:T(1,128)} %get-tuple-element.291) | copy-start | bytes 6148
  47.7 4.0 %copy-start.14 = (f32[8,4,64]{2,1,0:T(4,128)S(1)}, f32[8,4,64]{2,1,0:T(4,128)}, u32[]{:S(2)}) copy-start(f32[8,4,64]{2,1,0:T(4,128)} %copy.160) | copy-start | bytes 24580
  57.8 1.0 copy-start.7
  64.3 2.0 copy-start.1
  66.4 1.6 slice-start
  72.2 82.7 %copy-start.2 = (f32[8,4,128,256]{3,2,1,0:T(8,128)}, f32[8,4,128,256]{3,2,1,0:T(8,128)S(1)}, u32[]{:S(2)}) copy-start(f32[8,4,128,256]{3,2,1,0:T(8,128)S(1)} %pad_add_fusion) | copy-start | bytes 12582916
  72.3 13.2 %collective-permute-start.1 = (f32[4,128,128]{2,1,0:T(8,128)S(1)}, f32[4,128,128]{2,1,0:T(8,128)S(1)}, u32[]{:S(2)}, u32[]{:S(2)}) collective-permute-start(f32[4,128,128]{2,1,0:T(8,128)S(1)} %get-tuple-element.279), channel_id=1, source_target_pairs={{0,8},{8,16},{16,24},{24,32},{32,40},{40,48},{48,56},{56,64},{64,7... | collective-permute-start | bytes 786440 | tf_op jit(solution)/shard_map/ppermute | solution.py:17
  76.1 13.9 %collective-permute-start.2 = (f32[4,128,128]{2,1,0:T(8,128)S(1)}, f32[4,128,128]{2,1,0:T(8,128)S(1)}, u32[]{:S(2)}, u32[]{:S(2)}) collective-permute-start(f32[4,128,128]{2,1,0:T(8,128)S(1)} %get-tuple-element.280), channel_id=1, source_target_pairs={{0,8},{8,16},{16,24},{24,32},{32,40},{40,48},{48,56},{56,64},{64,7... | collective-permute-start | bytes 786440 | tf_op jit(solution)/shard_map/ppermute | solution.py:17
  90.5 24.2 %collective-permute-start.3 = (f32[4,128,128]{2,1,0:T(8,128)S(1)}, f32[4,128,128]{2,1,0:T(8,128)S(1)}, u32[]{:S(2)}, u32[]{:S(2)}) collective-permute-start(f32[4,128,128]{2,1,0:T(8,128)S(1)} %get-tuple-element.277), channel_id=1, source_target_pairs={{0,16},{8,24},{16,32},{24,40},{32,48},{40,56},{48,64},{56,72},{64,... | collective-permute-start | bytes 786440 | tf_op jit(solution)/shard_map/ppermute | solution.py:17
  93.8 24.8 %collective-permute-start.4 = (f32[4,128,128]{2,1,0:T(8,128)S(1)}, f32[4,128,128]{2,1,0:T(8,128)S(1)}, u32[]{:S(2)}, u32[]{:S(2)}) collective-permute-start(f32[4,128,128]{2,1,0:T(8,128)S(1)} %get-tuple-element.278), channel_id=1, source_target_pairs={{0,16},{8,24},{16,32},{24,40},{32,48},{40,56},{48,64},{56,72},{64,... | collective-permute-start | bytes 786440 | tf_op jit(solution)/shard_map/ppermute | solution.py:17
  119.0 35.9 %copy-start.15 = (f32[8,4,64]{2,0,1:T(8,128)S(1)}, f32[8,4,64]{2,0,1:T(8,128)}, u32[]{:S(2)}) copy-start(f32[8,4,64]{2,0,1:T(8,128)} %get-tuple-element.285) | copy-start | bytes 24580
  119.0 24.7 %collective-permute-start.5 = (f32[4,128,128]{2,1,0:T(8,128)S(1)}, f32[4,128,128]{2,1,0:T(8,128)S(1)}, u32[]{:S(2)}, u32[]{:S(2)}) collective-permute-start(f32[4,128,128]{2,1,0:T(8,128)S(1)} %get-tuple-element.275), channel_id=1, source_target_pairs={{0,32},{8,40},{16,48},{24,56},{32,64},{40,72},{48,80},{56,88},{64,... | collective-permute-start | bytes 786440 | tf_op jit(solution)/shard_map/ppermute | solution.py:17
  125.0 24.2 %collective-permute-start.6 = (f32[4,128,128]{2,1,0:T(8,128)S(1)}, f32[4,128,128]{2,1,0:T(8,128)S(1)}, u32[]{:S(2)}, u32[]{:S(2)}) collective-permute-start(f32[4,128,128]{2,1,0:T(8,128)S(1)} %get-tuple-element.276), channel_id=1, source_target_pairs={{0,32},{8,40},{16,48},{24,56},{32,64},{40,72},{48,80},{56,88},{64,... | collective-permute-start | bytes 786440 | tf_op jit(solution)/shard_map/ppermute | solution.py:17
  149.6 11.1 %collective-permute-start.7 = (f32[4,128,128]{2,1,0:T(8,128)S(1)}, f32[4,128,128]{2,1,0:T(8,128)S(1)}, u32[]{:S(2)}, u32[]{:S(2)}) collective-permute-start(f32[4,128,128]{2,1,0:T(8,128)S(1)} %get-tuple-element.273), channel_id=1, source_target_pairs={{0,64},{8,72},{16,80},{24,88},{32,96},{40,104},{48,112},{56,120},{... | collective-permute-start | bytes 786440 | tf_op jit(solution)/shard_map/ppermute | solution.py:17
  152.9 12.4 %collective-permute-start.8 = (f32[4,128,128]{2,1,0:T(8,128)S(1)}, f32[4,128,128]{2,1,0:T(8,128)S(1)}, u32[]{:S(2)}, u32[]{:S(2)}) collective-permute-start(f32[4,128,128]{2,1,0:T(8,128)S(1)} %get-tuple-element.274), channel_id=1, source_target_pairs={{0,64},{8,72},{16,80},{24,88},{32,96},{40,104},{48,112},{56,120},{... | collective-permute-start | bytes 786440 | tf_op jit(solution)/shard_map/ppermute | solution.py:17
  154.9 12.4 %copy-start.4 = (f32[8,4,128,64]{2,3,1,0:T(8,128)S(1)}, f32[8,4,128,64]{2,3,1,0:T(8,128)}, u32[]{:S(2)}) copy-start(f32[8,4,128,64]{2,3,1,0:T(8,128)} %copy-done.3) | copy-start | bytes 3145732
  165.7 13.2 %slice-start.1 = ((f32[8,4,128,256]{3,2,1,0:T(8,128)}), f32[7,4,128,256]{3,2,1,0:T(8,128)S(1)}, s32[]{:S(2)}) async-start(f32[8,4,128,256]{3,2,1,0:T(8,128)} %copy-done.2), calls=%async_computation.2 | async-start | bytes 7340032 | tf_op jit(solution)/shard_map/slice | solution.py:177
  165.7 13.2 %copy-start.6 = (f32[512,2,2,128]{3,0,2,1:T(8,128)S(1)}, f32[512,2,2,128]{3,0,2,1:T(8,128)}, u32[]{:S(2)}) copy-start(f32[512,2,2,128]{3,0,2,1:T(8,128)} %copy-done.5) | copy-start | bytes 3145732
  165.7 11.0 %collective-permute-start.9 = (f32[4,128,128]{2,1,0:T(8,128)S(1)}, f32[4,128,128]{2,1,0:T(8,128)S(1)}, u32[]{:S(2)}, u32[]{:S(2)}) collective-permute-start(f32[4,128,128]{2,1,0:T(8,128)S(1)} %slice_add_fusion.1), channel_id=1, source_target_pairs={{0,128},{8,136},{16,144},{24,152},{32,160},{40,168},{48,176},{56,1... | collective-permute-start | bytes 786440 | tf_op jit(solution)/shard_map/ppermute | solution.py:17
  177.0 10.5 %collective-permute-start.10 = (f32[4,128,128]{2,1,0:T(8,128)S(1)}, f32[4,128,128]{2,1,0:T(8,128)S(1)}, u32[]{:S(2)}, u32[]{:S(2)}) collective-permute-start(f32[4,128,128]{2,1,0:T(8,128)S(1)} %convolution_add_fusion), channel_id=1, source_target_pairs={{0,8},{8,16},{16,24},{24,32},{32,40},{40,48},{48,56},{56,64},{64,7... | collective-permute-start | bytes 786440 | tf_op jit(solution)/shard_map/ppermute | solution.py:17
  188.4 1.5 copy-start.9
  (8 other events, 6.6 us)
